TPU v7x, 256 devices: a whole 4x4x8 slice. The times are simulated.
256 devices in a mesh: grp: 4 (over x), blk: 64 (over z, y, core).
Axes of the slice: x: 4, y: 4, z: 8, core: 2. Of those that a mesh axis runs over, the one named last changes fastest.
Arguments:
- integrals: bfloat16 [4, 64, 10, 24, 128, 128], P('grp', 'blk'), may hold values from -6 to 6
- coefficients: bfloat16 [3072, 192], P('blk'), may hold values from -0.25 to 0.25
- tile_blocks: int32 [4, 64, 10, 2], P('grp', 'blk'), may hold values from 0 to 23
- block_owner: int32 [48], replicated, may hold values from 0 to 3, as said below
Outputs:
- owned: bfloat16 [96, 4, 4, 1536, 192], P('grp', None, None, 'blk')
Inputs may be any that keep to these rules, and one draw needn't show every extreme that they name: `block_owner`: each owner holds at most 24 ij blocks, and some owner holds exactly 24.
All inputs are finite; a program needn't handle non-finite values.
Results may differ from a plain program's by a relative error of at most 0.0049.
Values may be sent and summed in bfloat16 or wider, within the bound.
No kernel may reach another device: no remote copies, remote signals or barrier semaphores. Data moves between devices by JAX's collectives and lax.ppermute only.
A program may use at most 64 MiB of HBM per device.

v0:
```python
import jax
import jax.numpy as jnp
from jax import lax
from jax.sharding import PartitionSpec as P

NMO = 192
SB = 128
NSH = 24
R = 24
IJB = 48
CAP = 24
IPB = 4


def slot_table(block_owner, groups, capacity):
    count = block_owner.shape[0]
    order = jnp.arange(count, dtype=jnp.int32)
    same = block_owner[:, None] == block_owner[None, :]
    earlier = order[None, :] < order[:, None]
    rank = jnp.sum((same & earlier).astype(jnp.int32), axis=1)
    slot = block_owner * capacity + rank
    slots = jnp.arange(groups * capacity, dtype=jnp.int32)
    match = slot[None, :] == slots[:, None]
    source = jnp.sum(jnp.where(match, order[None, :], 0), axis=1)
    filled = jnp.any(match, axis=1)
    return (source, filled)


def body(integrals, coefficients, tile_blocks, block_owner):
    groups = lax.axis_size("grp")
    whole_coef = lax.all_gather(coefficients, "blk", axis=0, tiled=True)
    panels = whole_coef.reshape(NSH, SB, NMO)
    tiles = integrals[0, 0]
    blocks = tile_blocks[0, 0]
    la_coef = jnp.take(panels, blocks[:, 0], axis=0)
    si_coef = jnp.take(panels, blocks[:, 1], axis=0)
    quarter = jnp.einsum(
        "trab,tbj->tarj", tiles, si_coef, preferred_element_type=jnp.float32
    ).astype(jnp.bfloat16)
    half = jnp.einsum("tai,tarj->irj", la_coef, quarter, preferred_element_type=jnp.float32).astype(
        jnp.bfloat16
    )
    pair_blocks = half.reshape(IJB, IPB, R, NMO)
    source, filled = slot_table(block_owner, groups, CAP)
    everyone = lax.all_gather(pair_blocks[:, None], "grp", axis=1, tiled=True)
    mine = lax.axis_index("grp")
    wanted = lax.dynamic_slice_in_dim(source, mine * CAP, CAP, 0)
    present = lax.dynamic_slice_in_dim(filled, mine * CAP, CAP, 0)
    picked = jnp.take(everyone, wanted, axis=0)
    result = jnp.where(present[:, None, None, None, None], picked, jnp.zeros_like(picked))
    return result


def solution(mesh):
    in_specs = (
        P("grp", "blk", None, None, None, None),
        P("blk", None),
        P("grp", "blk", None, None),
        P(),
    )
    out_specs = P("grp", None, None, "blk", None)
    return jax.shard_map(body, mesh=mesh, in_specs=in_specs, out_specs=out_specs, check_vma=False)
```

profile of v0, /device:TPU:2, one launch (start us, length us, event | category | flops | bytes accessed | tf_op | source)
XLA Modules:
  0.0 215.8 jit_solution(501056608193168848)
XLA Ops:
  6.5 0.0 all-gather.3.cloned.1.call-start
  6.5 0.7 all-gather.3.cloned.1.call-update
  7.3 0.0 all-gather.5.cloned.1.call-start
  7.3 0.8 compare_and_fusion.1
  8.1 82.1 %all-gather.3.cloned.1.call-done = bf16[3072,192]{1,0:T(8,128)(2,1)} async-done(((bf16[48,192]{1,0:T(8,128)(2,1)}), bf16[3072,192]{1,0:T(8,128)(2,1)}) %all-gather.3.cloned.1.call-update) | async-done | bytes 1179664 | tf_op jit(solution)/shard_map/all_gather | solution.py:31
  90.2 1.9 copy.17
  92.0 0.6 gather_fusion.2
  92.7 0.6 gather_fusion.1
  93.3 8.7 %bitcast_convert_fusion = bf16[192,24,192]{2,0,1:T(8,128)(2,1)S(1)} fusion(bf16[10,128,192]{1,2,0:T(8,128)(2,1)S(1)} %gather_fusion.2, bf16[10,128,192]{1,2,0:T(8,128)(2,1)S(1)} %gather_fusion.1, pred[10]{0:T(512)(128)(4,1)S(1)} %get-tuple-element.12, pred[10]{0:T(512)(128)(4,1)S(1)} %get-tuple-element.8, bf16[1,1,10,24,128,128]{5,4,3,2,1,0:T(8,128)(2,1)} %param.6), kind=kOutput, calls=%fused_computation.8 | convolution fusion | flops 3782148096 | bytes 10616852 | tf_op jit(solution)/shard_map/tai,tarj->irj/dot_general | solution.py:40
  102.0 0.0 copy-start
  102.0 2.7 %copy.25 = bf16[192,24,192]{2,1,0:T(8,128)(2,1)} copy(bf16[192,24,192]{2,0,1:T(8,128)(2,1)S(1)} %bitcast_convert_fusion) | data formatting | bytes 3538944 | tf_op jit(solution)/shard_map/broadcast_in_dim;reshape | solution.py:45
  104.8 0.0 all-gather.5.cloned.1.call-update
  104.8 0.0 copy-done
  104.8 0.2 convert_reduce_fusion
  105.0 0.1 fusion.24
  105.1 0.1 dynamic_slice.6
  105.2 0.1 select_reduce_fusion
  105.3 0.1 compare_and_fusion.2
  105.4 91.7 %all-gather.5.cloned.1.call-done = bf16[48,4,4,24,192]{4,3,2,1,0:T(8,128)(2,1)} async-done(((bf16[48,1,4,24,192]{4,3,2,1,0:T(8,128)(2,1)}), bf16[48,4,4,24,192]{4,3,2,1,0:T(8,128)(2,1)}) %all-gather.5.cloned.1.call-update) | async-done | bytes 7077904 | tf_op jit(solution)/shard_map/all_gather | solution.py:45
  197.0 6.9 %gather_fusion = bf16[24,4,4,24,192]{4,3,2,1,0:T(8,128)(2,1)} fusion(bf16[48,4,4,24,192]{4,3,2,1,0:T(8,128)(2,1)} %all-gather.5.cloned.1.call-done, s32[1024]{0:T(1024)S(1)} %pad_clamp_fusion), kind=kCustom, calls=%fused_computation.2 | custom fusion | bytes 7077984 | tf_op jit(solution)/shard_map/jit(_take)/gather | solution.py:49
  203.9 5.1 %select_select_fusion = bf16[24,4,4,24,192]{4,3,2,1,0:T(8,128)(2,1)} fusion(bf16[24,4,4,24,192]{4,3,2,1,0:T(8,128)(2,1)} %gather_fusion, pred[24]{0:T(512)(128)(4,1)S(1)} %get-tuple-element.6, pred[24]{0:T(512)(128)(4,1)S(1)} %dynamic_slice.6), kind=kLoop, calls=%fused_computation.9 | loop fusion | flops 3538944 | bytes 7077936 | tf_op jit(solution)/shard_map/jit(_where)/select_n | solution.py:50
  (3 shorter events, 0.0 us)
Async XLA Ops:
  6.5 83.6 %all-gather.3.cloned.1.call-start = ((), (), s32[]{:S(2)}) async-start(), calls=%async_computation | async-start | bytes 1597440 | tf_op jit(solution)/shard_map/all_gather | solution.py:31
  7.3 189.8 %all-gather.5.cloned.1.call-start = ((), (), s32[]{:S(2)}) async-start(), calls=%async_computation.1 | async-start | bytes 11796480 | tf_op jit(solution)/shard_map/all_gather | solution.py:45
  102.0 2.8 %copy-start = (s32[48]{0:T(128)S(1)}, s32[48]{0:T(128)}, u32[]{:S(2)}) copy-start(s32[48]{0:T(128)} %param.9) | copy-start | bytes 580
Sparse Core Ops, SparseCore 0:
  10.1 80.0 all-gather.2
  104.9 92.0 all-gather.4
where the time goes:
time: 217 us; the launch traced here: 216 us
  waiting for transfers between devices  174 us (80%)
  between operations  13.5 us (6%)
  local copies, waits for them, and re-layouts  12.8 us (6%)
  matrix products  8.69 us (4%)
  other arithmetic  6.33 us (3%)
    all_gather x1, waiting for transfers between devices, body(): everyone = lax.all_gather(pair_blocks[:, None], 'grp', axis=1, tiled=True)  91.7 us
    all_gather x1, waiting for transfers between devices, body(): whole_coef = lax.all_gather(coefficients, 'blk', axis=0, tiled=True)  82.1 us
    dot_general x1, matrix products, body(): jnp.einsum('tai,tarj->irj', la_coef, quarter, preferred_element_type=jnp....  8.69 us
    gather x1, local copies, waits for them, and re-layouts, body(): picked = jnp.take(everyone, wanted, axis=0)  6.87 us
    select_n x1, other arithmetic, body(): jnp.where(present[:, None, None, None, None], picked, jnp.zeros_like(pick...  5.1 us
  transfers between devices with their start and end apart: 2, of which 2 were waited for; matrix products, arithmetic and copies ran while one was open for 1% of the time, Pallas kernels for 0%

commit v1 on v0

v1 whole, which is shorter than its diff:
```python
import numpy as np
import jax
import jax.numpy as jnp
from jax import lax
from jax.sharding import Mesh, PartitionSpec as P

NMO = 192
SB = 128
NSH = 24
R = 24
IJB = 48
CAP = 24
IPB = 4

BLK = ("z", "y", "c")


def slot_table(block_owner, groups, capacity):
    count = block_owner.shape[0]
    order = jnp.arange(count, dtype=jnp.int32)
    same = block_owner[:, None] == block_owner[None, :]
    earlier = order[None, :] < order[:, None]
    rank = jnp.sum((same & earlier).astype(jnp.int32), axis=1)
    slot = block_owner * capacity + rank
    slots = jnp.arange(groups * capacity, dtype=jnp.int32)
    match = slot[None, :] == slots[:, None]
    source = jnp.sum(jnp.where(match, order[None, :], 0), axis=1)
    filled = jnp.any(match, axis=1)
    return (source, filled)


def gather_coef(coefficients):
    x = lax.all_gather(coefficients, "c", axis=0, tiled=True)
    x = lax.all_gather(x, "y", axis=0, tiled=True)
    nz = lax.axis_size("z")
    rep = jnp.broadcast_to(x[None], (nz,) + x.shape)
    return lax.all_to_all(rep, "z", 0, 0, tiled=True).reshape(-1, NMO)


def body(integrals, coefficients, tile_blocks, block_owner):
    groups = lax.axis_size("grp")
    whole_coef = gather_coef(coefficients)
    panels = whole_coef.reshape(NSH, SB, NMO)
    tiles = integrals[0, 0]
    blocks = tile_blocks[0, 0]
    la_coef = jnp.take(panels, blocks[:, 0], axis=0)
    si_coef = jnp.take(panels, blocks[:, 1], axis=0)
    quarter = jnp.einsum(
        "trab,tbj->tarj", tiles, si_coef, preferred_element_type=jnp.float32
    ).astype(jnp.bfloat16)
    half = jnp.einsum("tai,tarj->irj", la_coef, quarter, preferred_element_type=jnp.float32).astype(
        jnp.bfloat16
    )
    pair_blocks = half.reshape(IJB, IPB, R, NMO)
    source, filled = slot_table(block_owner, groups, CAP)
    picked = jnp.take(pair_blocks, source, axis=0)
    picked = jnp.where(filled[:, None, None, None], picked, jnp.zeros_like(picked))
    return lax.all_to_all(picked[:, None], "grp", 0, 1, tiled=True)


def solution(mesh):
    nblk = mesh.shape["blk"]
    devs = np.asarray(mesh.devices).reshape(mesh.shape["grp"], nblk // 8, 4, 2)
    parts = Mesh(devs, ("grp",) + BLK)
    in_specs = (
        P("grp", BLK, None, None, None, None),
        P(BLK, None),
        P("grp", BLK, None, None),
        P(),
    )
    out_specs = P("grp", None, None, BLK, None)
    return jax.shard_map(body, mesh=parts, in_specs=in_specs, out_specs=out_specs, check_vma=False)
```

time: 217 us -> 134 us (0.62)
  waiting for transfers between devices: 174 us -> 26.2 us
  blocking collectives: 0 us -> 70.3 us
  between operations: 13.5 us -> 0.07 us
  starting transfers between devices: 0.04 us -> 8.47 us
    all_gather x2 -> x0, waiting for transfers between devices: 174 us -> none  [the longest x1 91.7 us: body(): everyone = lax.all_gather(pair_blocks[:, None], 'grp', axis=1, tiled=True)]
    all_to_all x0 -> x1, blocking collectives: none -> 55.6 us  [body(): return lax.all_to_all(picked[:, None], 'grp', 0, 1, tiled=True)]
    all_to_all x0 -> x1, waiting for transfers between devices: none -> 26.2 us  [gather_coef(): return lax.all_to_all(rep, 'z', 0, 0, tiled=True).reshape(-1, NMO)]
    all_gather x0 -> x2, blocking collectives: none -> 14.7 us  [the longest x1 12.6 us: gather_coef(): x = lax.all_gather(x, 'y', axis=0, tiled=True)]
    all_to_all x0 -> x1, starting transfers between devices: none -> 8.47 us  [gather_coef(): return lax.all_to_all(rep, 'z', 0, 0, tiled=True).reshape(-1, NMO)]
    gather x1, local copies, waits for them, and re-layouts: 6.87 us -> 3.23 us  [body(): picked = jnp.take(pair_blocks, source, axis=0)]
    all_to_all x0 -> x2, local copies, waits for them, and re-layouts: none -> 3.33 us  [the longest x1 2.64 us: body(): return lax.all_to_all(picked[:, None], 'grp', 0, 1, tiled=True)]
    select_n x1 -> x2, other arithmetic: 5.1 us -> 2.98 us  [the longest x1 2.97 us: body(): jnp.where(filled[:, None, None, None], picked, jnp.zeros_like(picked))]
  transfers between devices with their start and end apart: 2 -> 1, of which waited for: 2 -> 1; matrix products, arithmetic and copies ran while one was open for 1% -> 2% of each run, Pallas kernels for 0% -> 0%
where the time goes in v1:
time: 134 us
  blocking collectives  70.3 us (52%)
  waiting for transfers between devices  26.2 us (20%)
  local copies, waits for them, and re-layouts  12.9 us (10%)
  matrix products  9.68 us (7%)
  starting transfers between devices  8.47 us (6%)
  other arithmetic  6.12 us (5%)
    all_to_all x1, blocking collectives, body(): return lax.all_to_all(picked[:, None], 'grp', 0, 1, tiled=True)  55.6 us
    all_to_all x1, waiting for transfers between devices, gather_coef(): return lax.all_to_all(rep, 'z', 0, 0, tiled=True).reshape(-1, NMO)  26.2 us
    all_gather x1, blocking collectives, gather_coef(): x = lax.all_gather(x, 'y', axis=0, tiled=True)  12.6 us
    dot_general x1, matrix products, body(): jnp.einsum('tai,tarj->irj', la_coef, quarter, preferred_element_type=jnp....  9.68 us
    all_to_all x1, starting transfers between devices, gather_coef(): return lax.all_to_all(rep, 'z', 0, 0, tiled=True).reshape(-1, NMO)  8.47 us
    gather x1, local copies, waits for them, and re-layouts, body(): picked = jnp.take(pair_blocks, source, axis=0)  3.23 us
    reshape x1, local copies, waits for them, and re-layouts, body(): pair_blocks = half.reshape(IJB, IPB, R, NMO)  2.99 us
    select_n x1, other arithmetic, body(): jnp.where(filled[:, None, None, None], picked, jnp.zeros_like(picked))  2.97 us
  transfers between devices with their start and end apart: 1, of which 1 were waited for; matrix products, arithmetic and copies ran while one was open for 2% of the time, Pallas kernels for 0%

profile of v1, /device:TPU:2, one launch (start us, length us, event | category | flops | bytes accessed | tf_op | source)
XLA Modules:
  0.0 133.8 jit_solution(2959401392641210063)
XLA Ops:
  0.0 2.0 %all_gather.6 = bf16[96,192]{1,0:T(8,128)(2,1)S(1)} all-gather(bf16[48,192]{1,0:T(8,128)(2,1)} %param.7), channel_id=1, replica_groups=mesh['grp'=4,'z'=8,'y'=4,'c'=2] {'c'}, dimensions={0}, use_global_device_ids=true | all-gather | bytes 55296 | tf_op jit(solution)/shard_map/all_gather | solution.py:33
  2.0 12.6 %all_gather.7 = bf16[384,192]{1,0:T(8,128)(2,1)S(1)} all-gather(bf16[96,192]{1,0:T(8,128)(2,1)S(1)} %all_gather.6), channel_id=1, replica_groups=mesh['grp'=4,'z'=8,'y'=4,'c'=2] {'y'}, dimensions={0}, use_global_device_ids=true | all-gather | bytes 184320 | tf_op jit(solution)/shard_map/all_gather | solution.py:34
  14.7 0.1 copy.26
  14.8 1.1 broadcast_in_dim.61
  15.9 8.5 %all-to-all-start = ((bf16[8,384,192]{1,2,0:T(8,128)(2,1)}), bf16[8,384,192]{1,2,0:T(8,128)(2,1)S(1)}, u32[]{:S(2)}, u32[]{:S(2)}) async-start(bf16[8,384,192]{1,2,0:T(8,128)(2,1)} %broadcast_in_dim.61), calls=%async_computation | async-start | bytes 2359296 | tf_op jit(solution)/shard_map/all_to_all | solution.py:37
  24.4 0.9 convert_reduce_fusion
  25.3 0.7 multiply_add_fusion
  26.0 0.1 select_reduce_fusion
  26.1 0.8 compare_and_fusion.1
  26.9 0.1 fusion.26
  27.0 0.6 compare_and_fusion.2
  27.6 26.2 %all-to-all-done = bf16[8,384,192]{1,2,0:T(8,128)(2,1)S(1)} async-done(((bf16[8,384,192]{1,2,0:T(8,128)(2,1)}), bf16[8,384,192]{1,2,0:T(8,128)(2,1)S(1)}, u32[]{:S(2)}, u32[]{:S(2)}) %all-to-all-start) | async-done | bytes 1179680 | tf_op jit(solution)/shard_map/all_to_all | solution.py:37
  53.8 0.7 copy.27
  54.5 0.6 reshape_reshape.3
  55.1 0.2 copy.28
  55.3 0.6 gather_fusion.2
  56.0 0.6 gather_fusion.1
  56.6 9.7 %bitcast_convert_fusion = bf16[192,24,192]{2,0,1:T(8,128)(2,1)} fusion(bf16[10,128,192]{1,2,0:T(8,128)(2,1)S(1)} %gather_fusion.2, bf16[10,128,192]{1,2,0:T(8,128)(2,1)S(1)} %gather_fusion.1, pred[10]{0:T(512)(128)(4,1)S(1)} %get-tuple-element.10, pred[10]{0:T(512)(128)(4,1)S(1)} %get-tuple-element.6, bf16[1,1,10,24,128,128]{5,4,3,2,1,0:T(8,128)(2,1)} %param.6), kind=kOutput, calls=%fused_computation.11 | convolution fusion | flops 3782148096 | bytes 10616852 | tf_op jit(solution)/shard_map/tai,tarj->irj/dot_general | solution.py:51
  66.3 3.0 %copy.35 = bf16[192,24,192]{2,1,0:T(8,128)(2,1)S(1)} copy(bf16[192,24,192]{2,0,1:T(8,128)(2,1)} %bitcast_convert_fusion) | data formatting | bytes 3538944 | tf_op jit(solution)/shard_map/reshape | solution.py:54
  69.3 0.0 copy-start
  69.3 3.2 %gather_fusion = bf16[96,4,24,192]{3,2,1,0:T(8,128)(2,1)} fusion(bf16[48,4,24,192]{3,2,1,0:T(8,128)(2,1)S(1)} %bitcast.47, s32[1024]{0:T(1024)S(1)} %pad_clamp_fusion), kind=kCustom, calls=%fused_computation.2 | custom fusion | bytes 7078272 | tf_op jit(solution)/shard_map/jit(_take)/gather | solution.py:56
  72.5 3.0 %fusion.10 = bf16[96,1,4,24,192]{4,3,2,1,0:T(8,128)(2,1)S(1)} fusion(bf16[96,4,24,192]{3,2,1,0:T(8,128)(2,1)} %gather_fusion, pred[96]{0:T(512)(128)(4,1)S(1)} %copy-done, pred[96]{0:T(512)(128)(4,1)S(1)} %fusion.26), kind=kLoop, calls=%fused_computation.10 | loop fusion | flops 3538944 | bytes 7078080 | tf_op jit(solution)/shard_map/jit(_where)/select_n | solution.py:57
  75.5 55.6 %all_to_all.23 = bf16[96,1,4,24,192]{4,3,2,1,0:T(8,128)(2,1)S(1)} all-to-all(bf16[96,1,4,24,192]{4,3,2,1,0:T(8,128)(2,1)S(1)} %fusion.10), channel_id=1, replica_groups=mesh['grp'=4,'z'=8,'y'=4,'c'=2] {'grp'}, dimensions={0} | all-to-all | bytes 7077888 | tf_op jit(solution)/shard_map/all_to_all | solution.py:58
  131.1 2.6 %copy.33 = bf16[24,4,4,24,192]{4,3,2,1,0:T(8,128)(2,1)} copy(bf16[24,4,4,24,192]{4,3,2,0,1:T(8,128)(2,1)S(1)} %bitcast.48) | data formatting | bytes 7077888 | tf_op jit(solution)/shard_map/all_to_all | solution.py:58
  (4 shorter events, 0.0 us)
Async XLA Ops:
  15.9 37.8 %all-to-all-start = ((bf16[8,384,192]{1,2,0:T(8,128)(2,1)}), bf16[8,384,192]{1,2,0:T(8,128)(2,1)S(1)}, u32[]{:S(2)}, u32[]{:S(2)}) async-start(bf16[8,384,192]{1,2,0:T(8,128)(2,1)} %broadcast_in_dim.61), calls=%async_computation | async-start | bytes 2359296 | tf_op jit(solution)/shard_map/all_to_all | solution.py:37
  69.3 3.2 %copy-start = (pred[96]{0:T(512)(128)(4,1)S(1)}, pred[96]{0:T(512)(128)(4,1)}, u32[]{:S(2)}) copy-start(pred[96]{0:T(512)(128)(4,1)} %compare_and_fusion.2) | copy-start | bytes 292

commit v2 on v1

--- a/solution.py
+++ b/solution.py
@@ -29,20 +29,38 @@
     return (source, filled)
 
 
+def ring(x, axis):
+    n = lax.axis_size(axis)
+    got = {0: x}
+    f = x
+    for k in range(1, n // 2 + 1):
+        f = lax.ppermute(f, axis, [(s, (s + 1) % n) for s in range(n)])
+        got[-k] = f
+    b = x
+    for k in range(1, n - n // 2):
+        b = lax.ppermute(b, axis, [(s, (s - 1) % n) for s in range(n)])
+        got[k] = b
+    lo = -(n // 2)
+    return jnp.stack([got[o] for o in range(lo, lo + n)]), lo
+
+
 def gather_coef(coefficients):
     x = lax.all_gather(coefficients, "c", axis=0, tiled=True)
-    x = lax.all_gather(x, "y", axis=0, tiled=True)
-    nz = lax.axis_size("z")
-    rep = jnp.broadcast_to(x[None], (nz,) + x.shape)
-    return lax.all_to_all(rep, "z", 0, 0, tiled=True).reshape(-1, NMO)
+    ny = lax.axis_size("y")
+    stack, lo = ring(x, "y")
+    want = (jnp.arange(ny) - lax.axis_index("y") - lo) % ny
+    x = jnp.take(stack, want, axis=0).reshape(-1, NMO)
+    stack, lo = ring(x, "z")
+    per = NSH // lax.axis_size("z")
+    return stack.reshape(-1, NMO), per * (lax.axis_index("z") + lo)
 
 
 def body(integrals, coefficients, tile_blocks, block_owner):
     groups = lax.axis_size("grp")
-    whole_coef = gather_coef(coefficients)
+    whole_coef, shift = gather_coef(coefficients)
     panels = whole_coef.reshape(NSH, SB, NMO)
     tiles = integrals[0, 0]
-    blocks = tile_blocks[0, 0]
+    blocks = (tile_blocks[0, 0] - shift) % NSH
     la_coef = jnp.take(panels, blocks[:, 0], axis=0)
     si_coef = jnp.take(panels, blocks[:, 1], axis=0)
     quarter = jnp.einsum(

time: 134 us -> 124 us (0.925)
  blocking collectives: 70.3 us -> 53.3 us
  starting transfers between devices: 8.47 us -> 15.2 us
    all_to_all x1 -> x0, waiting for transfers between devices: 26.2 us -> none  [gather_coef(): return lax.all_to_all(rep, 'z', 0, 0, tiled=True).reshape(-1, NMO)]
    ppermute x0 -> x10, waiting for transfers between devices: none -> 25.7 us  [the longest x6 25.7 us: ring(): f = lax.ppermute(f, axis, [(s, (s + 1) % n) for s in range(n)])]
    ppermute x0 -> x10, starting transfers between devices: none -> 15.2 us  [the longest x4 13.2 us: ring(): b = lax.ppermute(b, axis, [(s, (s - 1) % n) for s in range(n)])]
    all_gather x1 -> x0, blocking collectives: 12.6 us -> none  [gather_coef(): x = lax.all_gather(x, 'y', axis=0, tiled=True)]
    all_to_all x1 -> x0, starting transfers between devices: 8.47 us -> none  [gather_coef(): return lax.all_to_all(rep, 'z', 0, 0, tiled=True).reshape(-1, NMO)]
    all_to_all x1, blocking collectives: 55.6 us -> 51.2 us  [body(): return lax.all_to_all(picked[:, None], 'grp', 0, 1, tiled=True)]
  transfers between devices with their start and end apart: 1 -> 10, of which waited for: 1 -> 6; matrix products, arithmetic and copies ran while one was open for 2% -> 2% of each run, Pallas kernels for 0% -> 0%
where the time goes in v2:
time: 124 us; the launch traced here: 123 us
  blocking collectives  53.3 us (43%)
  waiting for transfers between devices  25.7 us (21%)
  starting transfers between devices  15.2 us (12%)
  local copies, waits for them, and re-layouts  12.8 us (10%)
  matrix products  9.68 us (8%)
  other arithmetic  5.6 us (5%)
    all_to_all x1, blocking collectives, body(): return lax.all_to_all(picked[:, None], 'grp', 0, 1, tiled=True)  51.2 us
    ppermute x6, waiting for transfers between devices, ring(): f = lax.ppermute(f, axis, [(s, (s + 1) % n) for s in range(n)])  25.7 us
    ppermute x4, starting transfers between devices, ring(): b = lax.ppermute(b, axis, [(s, (s - 1) % n) for s in range(n)])  13.2 us
    dot_general x1, matrix products, body(): jnp.einsum('tai,tarj->irj', la_coef, quarter, preferred_element_type=jnp....  9.68 us
    gather x1, local copies, waits for them, and re-layouts, body(): picked = jnp.take(pair_blocks, source, axis=0)  3.23 us
    reshape x1, local copies, waits for them, and re-layouts, body(): pair_blocks = half.reshape(IJB, IPB, R, NMO)  2.99 us
    select_n x1, other arithmetic, body(): jnp.where(filled[:, None, None, None], picked, jnp.zeros_like(picked))  2.97 us
    all_to_all x1, local copies, waits for them, and re-layouts, body(): return lax.all_to_all(picked[:, None], 'grp', 0, 1, tiled=True)  2.64 us
  transfers between devices with their start and end apart: 10, of which 6 were waited for; matrix products, arithmetic and copies ran while one was open for 2% of the time, Pallas kernels for 0%

profile of v2, /device:TPU:2, one launch (start us, length us, event | category | flops | bytes accessed | tf_op | source)
XLA Modules:
  0.0 122.5 jit_solution(15563558308107269913)
XLA Ops:
  0.0 2.0 %all_gather.3 = bf16[96,192]{1,0:T(8,128)(2,1)S(1)} all-gather(bf16[48,192]{1,0:T(8,128)(2,1)} %param.7), channel_id=1, replica_groups=mesh['grp'=4,'z'=8,'y'=4,'c'=2] {'c'}, dimensions={0}, use_global_device_ids=true | all-gather | bytes 55296 | tf_op jit(solution)/shard_map/all_gather | solution.py:48
  2.0 3.1 %collective-permute-start.2 = (bf16[96,192]{1,0:T(8,128)(2,1)S(1)}, bf16[96,192]{1,0:T(8,128)(2,1)S(1)}, u32[]{:S(2)}, u32[]{:S(2)}) collective-permute-start(bf16[96,192]{1,0:T(8,128)(2,1)S(1)} %all_gather.3), channel_id=1, source_target_pairs={{0,6},{2,0},{4,2},{6,4},{1,7},{3,1},{5,3},{7,5},{8,14},{10,8},{12,... | collective-permute-start | bytes 110600 | tf_op jit(solution)/shard_map/ppermute | solution.py:41
  5.1 0.9 convert_reduce_fusion
  6.1 0.7 and_select_fusion
  6.8 3.6 %collective-permute-done = bf16[96,192]{1,0:T(8,128)(2,1)S(1)} collective-permute-done((bf16[96,192]{1,0:T(8,128)(2,1)S(1)}, bf16[96,192]{1,0:T(8,128)(2,1)S(1)}, u32[]{:S(2)}, u32[]{:S(2)}) %collective-permute-start) | collective-permute-done | bytes 36896 | tf_op jit(solution)/shard_map/ppermute | solution.py:37
  10.6 5.1 %collective-permute-done.1 = bf16[96,192]{1,0:T(8,128)(2,1)S(1)} collective-permute-done((bf16[96,192]{1,0:T(8,128)(2,1)S(1)}, bf16[96,192]{1,0:T(8,128)(2,1)S(1)}, u32[]{:S(2)}, u32[]{:S(2)}) %collective-permute-start.1) | collective-permute-done | bytes 36896 | tf_op jit(solution)/shard_map/ppermute | solution.py:37
  16.5 2.0 %collective-permute-start.3 = (bf16[384,192]{0,1:T(8,128)(2,1)S(1)}, bf16[384,192]{0,1:T(8,128)(2,1)S(1)}, u32[]{:S(2)}, u32[]{:S(2)}) collective-permute-start(bf16[384,192]{0,1:T(8,128)(2,1)S(1)} %broadcast_select_fusion), channel_id=1, source_target_pairs={{0,8},{8,16},{16,24},{24,32},{32,40},{40,48},{48,56},{56,0},{1,9},... | collective-permute-start | bytes 442376 | tf_op jit(solution)/shard_map/ppermute | solution.py:37
  18.5 0.7 multiply_add_fusion
  19.3 6.3 %collective-permute-done.3 = bf16[384,192]{0,1:T(8,128)(2,1)S(1)} collective-permute-done((bf16[384,192]{0,1:T(8,128)(2,1)S(1)}, bf16[384,192]{0,1:T(8,128)(2,1)S(1)}, u32[]{:S(2)}, u32[]{:S(2)}) %collective-permute-start.3) | collective-permute-done | bytes 147488 | tf_op jit(solution)/shard_map/ppermute | solution.py:37
  25.6 3.2 %collective-permute-start.7 = (bf16[384,192]{0,1:T(8,128)(2,1)S(1)}, bf16[384,192]{0,1:T(8,128)(2,1)S(1)}, u32[]{:S(2)}, u32[]{:S(2)}) collective-permute-start(bf16[384,192]{0,1:T(8,128)(2,1)S(1)} %broadcast_select_fusion), channel_id=1, source_target_pairs={{0,56},{8,0},{16,8},{24,16},{32,24},{40,32},{48,40},{56,48},{1,57}... | collective-permute-start | bytes 442376 | tf_op jit(solution)/shard_map/ppermute | solution.py:41
  28.8 3.8 %collective-permute-done.4 = bf16[384,192]{0,1:T(8,128)(2,1)S(1)} collective-permute-done((bf16[384,192]{0,1:T(8,128)(2,1)S(1)}, bf16[384,192]{0,1:T(8,128)(2,1)S(1)}, u32[]{:S(2)}, u32[]{:S(2)}) %collective-permute-start.4) | collective-permute-done | bytes 147488 | tf_op jit(solution)/shard_map/ppermute | solution.py:37
  32.6 3.4 %collective-permute-start.8 = (bf16[384,192]{0,1:T(8,128)(2,1)S(1)}, bf16[384,192]{0,1:T(8,128)(2,1)S(1)}, u32[]{:S(2)}, u32[]{:S(2)}) collective-permute-start(bf16[384,192]{0,1:T(8,128)(2,1)S(1)} %collective-permute-done.7), channel_id=1, source_target_pairs={{0,56},{8,0},{16,8},{24,16},{32,24},{40,32},{48,40},{56,48},{1,57}... | collective-permute-start | bytes 442376 | tf_op jit(solution)/shard_map/ppermute | solution.py:41
  36.0 4.2 %collective-permute-done.5 = bf16[384,192]{0,1:T(8,128)(2,1)S(1)} collective-permute-done((bf16[384,192]{0,1:T(8,128)(2,1)S(1)}, bf16[384,192]{0,1:T(8,128)(2,1)S(1)}, u32[]{:S(2)}, u32[]{:S(2)}) %collective-permute-start.5) | collective-permute-done | bytes 147488 | tf_op jit(solution)/shard_map/ppermute | solution.py:37
  40.5 3.5 %collective-permute-start.9 = (bf16[384,192]{0,1:T(8,128)(2,1)S(1)}, bf16[384,192]{0,1:T(8,128)(2,1)S(1)}, u32[]{:S(2)}, u32[]{:S(2)}) collective-permute-start(bf16[384,192]{0,1:T(8,128)(2,1)S(1)} %collective-permute-done.8), channel_id=1, source_target_pairs={{0,56},{8,0},{16,8},{24,16},{32,24},{40,32},{48,40},{56,48},{1,57}... | collective-permute-start | bytes 442376 | tf_op jit(solution)/shard_map/ppermute | solution.py:41
  44.0 2.6 %collective-permute-done.6 = bf16[384,192]{0,1:T(8,128)(2,1)S(1)} collective-permute-done((bf16[384,192]{0,1:T(8,128)(2,1)S(1)}, bf16[384,192]{0,1:T(8,128)(2,1)S(1)}, u32[]{:S(2)}, u32[]{:S(2)}) %collective-permute-start.6) | collective-permute-done | bytes 147488 | tf_op jit(solution)/shard_map/ppermute | solution.py:37
  46.9 0.7 copy.38
  48.5 0.6 gather_fusion.3
  49.1 0.6 gather_fusion.2
  49.8 9.7 %bitcast_convert_fusion = bf16[192,24,192]{2,0,1:T(8,128)(2,1)} fusion(bf16[10,128,192]{1,2,0:T(8,128)(2,1)S(1)} %gather_fusion.3, bf16[10,128,192]{1,2,0:T(8,128)(2,1)S(1)} %gather_fusion.2, pred[10]{0:T(512)(128)(4,1)S(1)} %get-tuple-element.10, pred[10]{0:T(512)(128)(4,1)S(1)} %get-tuple-element.6, bf16[1,1,10,24,128,128]{5,4,3,2,1,0:T(8,128)(2,1)} %param.6), kind=kOutput, calls=%fused_computation.12 | convolution fusion | flops 3782148096 | bytes 10616852 | tf_op jit(solution)/shard_map/tai,tarj->irj/dot_general | solution.py:69
  59.4 3.0 %copy.48 = bf16[192,24,192]{2,1,0:T(8,128)(2,1)S(1)} copy(bf16[192,24,192]{2,0,1:T(8,128)(2,1)} %bitcast_convert_fusion) | data formatting | bytes 3538944 | tf_op jit(solution)/shard_map/reshape | solution.py:72
  62.4 3.2 %gather_fusion.1 = bf16[96,4,24,192]{3,2,1,0:T(8,128)(2,1)} fusion(bf16[48,4,24,192]{3,2,1,0:T(8,128)(2,1)S(1)} %bitcast.70, s32[1024]{0:T(1024)S(1)} %get-tuple-element.12), kind=kCustom, calls=%fused_computation.3 | custom fusion | bytes 7078272 | tf_op jit(solution)/shard_map/jit(_take)/gather | solution.py:74
  65.7 3.0 %fusion.10 = bf16[96,1,4,24,192]{4,3,2,1,0:T(8,128)(2,1)S(1)} fusion(bf16[96,4,24,192]{3,2,1,0:T(8,128)(2,1)} %gather_fusion.1, pred[96]{0:T(512)(128)(4,1)S(1)} %compare_and_fusion.3, pred[96]{0:T(512)(128)(4,1)S(1)} %fusion.26), kind=kLoop, calls=%fused_computation.11 | loop fusion | flops 3538944 | bytes 7078080 | tf_op jit(solution)/shard_map/jit(_where)/select_n | solution.py:75
  68.6 51.2 %all_to_all.18 = bf16[96,1,4,24,192]{4,3,2,1,0:T(8,128)(2,1)S(1)} all-to-all(bf16[96,1,4,24,192]{4,3,2,1,0:T(8,128)(2,1)S(1)} %fusion.10), channel_id=1, replica_groups=mesh['grp'=4,'z'=8,'y'=4,'c'=2] {'grp'}, dimensions={0} | all-to-all | bytes 7077888 | tf_op jit(solution)/shard_map/all_to_all | solution.py:76
  119.9 2.6 %copy.44 = bf16[24,4,4,24,192]{4,3,2,1,0:T(8,128)(2,1)} copy(bf16[24,4,4,24,192]{4,3,2,0,1:T(8,128)(2,1)S(1)} %bitcast.71) | data formatting | bytes 7077888 | tf_op jit(solution)/shard_map/all_to_all | solution.py:76
  (36 shorter events, 2.4 us)
Async XLA Ops:
  2.0 8.6 %collective-permute-start.2 = (bf16[96,192]{1,0:T(8,128)(2,1)S(1)}, bf16[96,192]{1,0:T(8,128)(2,1)S(1)}, u32[]{:S(2)}, u32[]{:S(2)}) collective-permute-start(bf16[96,192]{1,0:T(8,128)(2,1)S(1)} %all_gather.3), channel_id=1, source_target_pairs={{0,6},{2,0},{4,2},{6,4},{1,7},{3,1},{5,3},{7,5},{8,14},{10,8},{12,... | collective-permute-start | bytes 110600 | tf_op jit(solution)/shard_map/ppermute | solution.py:41
  5.1 5.3 %collective-permute-start = (bf16[96,192]{1,0:T(8,128)(2,1)S(1)}, bf16[96,192]{1,0:T(8,128)(2,1)S(1)}, u32[]{:S(2)}, u32[]{:S(2)}) collective-permute-start(bf16[96,192]{1,0:T(8,128)(2,1)S(1)} %all_gather.3), channel_id=1, source_target_pairs={{0,2},{2,4},{4,6},{6,0},{1,3},{3,5},{5,7},{7,1},{8,10},{10,12},{12... | collective-permute-start | bytes 110600 | tf_op jit(solution)/shard_map/ppermute | solution.py:37
  10.4 5.3 %collective-permute-start.1 = (bf16[96,192]{1,0:T(8,128)(2,1)S(1)}, bf16[96,192]{1,0:T(8,128)(2,1)S(1)}, u32[]{:S(2)}, u32[]{:S(2)}) collective-permute-start(bf16[96,192]{1,0:T(8,128)(2,1)S(1)} %collective-permute-done), channel_id=1, source_target_pairs={{0,2},{2,4},{4,6},{6,0},{1,3},{3,5},{5,7},{7,1},{8,10},{10,12},{12... | collective-permute-start | bytes 110600 | tf_op jit(solution)/shard_map/ppermute | solution.py:37
  16.5 9.1 %collective-permute-start.3 = (bf16[384,192]{0,1:T(8,128)(2,1)S(1)}, bf16[384,192]{0,1:T(8,128)(2,1)S(1)}, u32[]{:S(2)}, u32[]{:S(2)}) collective-permute-start(bf16[384,192]{0,1:T(8,128)(2,1)S(1)} %broadcast_select_fusion), channel_id=1, source_target_pairs={{0,8},{8,16},{16,24},{24,32},{32,40},{40,48},{48,56},{56,0},{1,9},... | collective-permute-start | bytes 442376 | tf_op jit(solution)/shard_map/ppermute | solution.py:37
  25.6 7.0 %collective-permute-start.4 = (bf16[384,192]{0,1:T(8,128)(2,1)S(1)}, bf16[384,192]{0,1:T(8,128)(2,1)S(1)}, u32[]{:S(2)}, u32[]{:S(2)}) collective-permute-start(bf16[384,192]{0,1:T(8,128)(2,1)S(1)} %collective-permute-done.3), channel_id=1, source_target_pairs={{0,8},{8,16},{16,24},{24,32},{32,40},{40,48},{48,56},{56,0},{1,9},... | collective-permute-start | bytes 442376 | tf_op jit(solution)/shard_map/ppermute | solution.py:37
  25.6 7.0 %collective-permute-start.7 = (bf16[384,192]{0,1:T(8,128)(2,1)S(1)}, bf16[384,192]{0,1:T(8,128)(2,1)S(1)}, u32[]{:S(2)}, u32[]{:S(2)}) collective-permute-start(bf16[384,192]{0,1:T(8,128)(2,1)S(1)} %broadcast_select_fusion), channel_id=1, source_target_pairs={{0,56},{8,0},{16,8},{24,16},{32,24},{40,32},{48,40},{56,48},{1,57}... | collective-permute-start | bytes 442376 | tf_op jit(solution)/shard_map/ppermute | solution.py:41
  32.6 7.7 %collective-permute-start.5 = (bf16[384,192]{0,1:T(8,128)(2,1)S(1)}, bf16[384,192]{0,1:T(8,128)(2,1)S(1)}, u32[]{:S(2)}, u32[]{:S(2)}) collective-permute-start(bf16[384,192]{0,1:T(8,128)(2,1)S(1)} %collective-permute-done.4), channel_id=1, source_target_pairs={{0,8},{8,16},{16,24},{24,32},{32,40},{40,48},{48,56},{56,0},{1,9},... | collective-permute-start | bytes 442376 | tf_op jit(solution)/shard_map/ppermute | solution.py:37
  32.6 7.9 %collective-permute-start.8 = (bf16[384,192]{0,1:T(8,128)(2,1)S(1)}, bf16[384,192]{0,1:T(8,128)(2,1)S(1)}, u32[]{:S(2)}, u32[]{:S(2)}) collective-permute-start(bf16[384,192]{0,1:T(8,128)(2,1)S(1)} %collective-permute-done.7), channel_id=1, source_target_pairs={{0,56},{8,0},{16,8},{24,16},{32,24},{40,32},{48,40},{56,48},{1,57}... | collective-permute-start | bytes 442376 | tf_op jit(solution)/shard_map/ppermute | solution.py:41
  40.3 6.4 %collective-permute-start.6 = (bf16[384,192]{0,1:T(8,128)(2,1)S(1)}, bf16[384,192]{0,1:T(8,128)(2,1)S(1)}, u32[]{:S(2)}, u32[]{:S(2)}) collective-permute-start(bf16[384,192]{0,1:T(8,128)(2,1)S(1)} %collective-permute-done.5), channel_id=1, source_target_pairs={{0,8},{8,16},{16,24},{24,32},{32,40},{40,48},{48,56},{56,0},{1,9},... | collective-permute-start | bytes 442376 | tf_op jit(solution)/shard_map/ppermute | solution.py:37
  40.5 6.3 %collective-permute-start.9 = (bf16[384,192]{0,1:T(8,128)(2,1)S(1)}, bf16[384,192]{0,1:T(8,128)(2,1)S(1)}, u32[]{:S(2)}, u32[]{:S(2)}) collective-permute-start(bf16[384,192]{0,1:T(8,128)(2,1)S(1)} %collective-permute-done.8), channel_id=1, source_target_pairs={{0,56},{8,0},{16,8},{24,16},{32,24},{40,32},{48,40},{56,48},{1,57}... | collective-permute-start | bytes 442376 | tf_op jit(solution)/shard_map/ppermute | solution.py:41

commit v3 on v2

--- a/solution.py
+++ b/solution.py
@@ -61,18 +61,19 @@
     panels = whole_coef.reshape(NSH, SB, NMO)
     tiles = integrals[0, 0]
     blocks = (tile_blocks[0, 0] - shift) % NSH
-    la_coef = jnp.take(panels, blocks[:, 0], axis=0)
-    si_coef = jnp.take(panels, blocks[:, 1], axis=0)
+    la_coef = jnp.take(panels, blocks[:, 0], axis=0, mode="clip")
+    si_coef = jnp.take(panels, blocks[:, 1], axis=0, mode="clip")
+    la_coef = jnp.pad(la_coef, ((0, 0), (0, 0), (0, IPB)))
     quarter = jnp.einsum(
         "trab,tbj->tarj", tiles, si_coef, preferred_element_type=jnp.float32
     ).astype(jnp.bfloat16)
     half = jnp.einsum("tai,tarj->irj", la_coef, quarter, preferred_element_type=jnp.float32).astype(
         jnp.bfloat16
     )
-    pair_blocks = half.reshape(IJB, IPB, R, NMO)
+    pair_blocks = half.reshape(IJB + 1, IPB, R, NMO)
     source, filled = slot_table(block_owner, groups, CAP)
-    picked = jnp.take(pair_blocks, source, axis=0)
-    picked = jnp.where(filled[:, None, None, None], picked, jnp.zeros_like(picked))
+    source = jnp.where(filled, source, IJB)
+    picked = jnp.take(pair_blocks, source, axis=0, mode="clip")
     return lax.all_to_all(picked[:, None], "grp", 0, 1, tiled=True)
 
 

time: 124 us -> 122 us (0.984)
  other arithmetic: 5.6 us -> 1.95 us
    convert_element_type x0 -> x1, local copies, waits for them, and re-layouts: none -> 3.87 us  [body(): jnp.einsum('tai,tarj->irj', la_coef, quarter, preferred_element_type=jnp....]
    reshape x1 -> x0, local copies, waits for them, and re-layouts: 2.99 us -> none  [body(): pair_blocks = half.reshape(IJB, IPB, R, NMO)]
    select_n x2 -> x1, other arithmetic: 2.97 us -> 0.01 us  [body(): source = jnp.where(filled, source, IJB)]
  transfers between devices with their start and end apart: 10 -> 10, of which waited for: 6 -> 7; matrix products, arithmetic and copies ran while one was open for 2% -> 2% of each run, Pallas kernels for 0% -> 0%
where the time goes in v3:
time: 122 us; the launch traced here: 121 us
  blocking collectives  53.6 us (44%)
  waiting for transfers between devices  26 us (21%)
  starting transfers between devices  15.6 us (13%)
  local copies, waits for them, and re-layouts  13.7 us (11%)
  matrix products  9.68 us (8%)
  other arithmetic  1.95 us (2%)
    all_to_all x1, blocking collectives, body(): return lax.all_to_all(picked[:, None], 'grp', 0, 1, tiled=True)  51.5 us
    ppermute x6, waiting for transfers between devices, ring(): f = lax.ppermute(f, axis, [(s, (s + 1) % n) for s in range(n)])  26 us
    ppermute x4, starting transfers between devices, ring(): b = lax.ppermute(b, axis, [(s, (s - 1) % n) for s in range(n)])  13.5 us
    dot_general x1, matrix products, body(): jnp.einsum('tai,tarj->irj', la_coef, quarter, preferred_element_type=jnp....  9.68 us
    convert_element_type x1, local copies, waits for them, and re-layouts, body(): jnp.einsum('tai,tarj->irj', la_coef, quarter, preferred_element_type=jnp....  3.87 us
    gather x1, local copies, waits for them, and re-layouts, body(): picked = jnp.take(pair_blocks, source, axis=0, mode='clip')  3.23 us
    all_to_all x1, local copies, waits for them, and re-layouts, body(): return lax.all_to_all(picked[:, None], 'grp', 0, 1, tiled=True)  2.64 us
  transfers between devices with their start and end apart: 10, of which 7 were waited for; matrix products, arithmetic and copies ran while one was open for 2% of the time, Pallas kernels for 0%

profile of v3, /device:TPU:2, one launch (start us, length us, event | category | flops | bytes accessed | tf_op | source)
XLA Modules:
  0.0 120.8 jit_solution(4602588184939321283)
XLA Ops:
  0.0 2.2 %all_gather.3 = bf16[96,192]{1,0:T(8,128)(2,1)S(1)} all-gather(bf16[48,192]{1,0:T(8,128)(2,1)} %param.5), channel_id=1, replica_groups=mesh['grp'=4,'z'=8,'y'=4,'c'=2] {'c'}, dimensions={0}, use_global_device_ids=true | all-gather | bytes 55296 | tf_op jit(solution)/shard_map/all_gather | solution.py:48
  2.2 3.1 %collective-permute-start.2 = (bf16[96,192]{1,0:T(8,128)(2,1)S(1)}, bf16[96,192]{1,0:T(8,128)(2,1)S(1)}, u32[]{:S(2)}, u32[]{:S(2)}) collective-permute-start(bf16[96,192]{1,0:T(8,128)(2,1)S(1)} %all_gather.3), channel_id=1, source_target_pairs={{0,6},{2,0},{4,2},{6,4},{1,7},{3,1},{5,3},{7,5},{8,14},{10,8},{12,... | collective-permute-start | bytes 110600 | tf_op jit(solution)/shard_map/ppermute | solution.py:41
  5.2 0.7 and_select_fusion
  5.9 0.9 convert_reduce_fusion
  6.9 3.7 %collective-permute-done = bf16[96,192]{1,0:T(8,128)(2,1)S(1)} collective-permute-done((bf16[96,192]{1,0:T(8,128)(2,1)S(1)}, bf16[96,192]{1,0:T(8,128)(2,1)S(1)}, u32[]{:S(2)}, u32[]{:S(2)}) %collective-permute-start) | collective-permute-done | bytes 36896 | tf_op jit(solution)/shard_map/ppermute | solution.py:37
  10.7 5.1 %collective-permute-done.1 = bf16[96,192]{1,0:T(8,128)(2,1)S(1)} collective-permute-done((bf16[96,192]{1,0:T(8,128)(2,1)S(1)}, bf16[96,192]{1,0:T(8,128)(2,1)S(1)}, u32[]{:S(2)}, u32[]{:S(2)}) %collective-permute-start.1) | collective-permute-done | bytes 36896 | tf_op jit(solution)/shard_map/ppermute | solution.py:37
  15.9 0.6 gather_fusion
  16.6 2.0 %collective-permute-start.3 = (bf16[384,192]{0,1:T(8,128)(2,1)S(1)}, bf16[384,192]{0,1:T(8,128)(2,1)S(1)}, u32[]{:S(2)}, u32[]{:S(2)}) collective-permute-start(bf16[384,192]{0,1:T(8,128)(2,1)S(1)} %broadcast_select_fusion), channel_id=1, source_target_pairs={{0,8},{8,16},{16,24},{24,32},{32,40},{40,48},{48,56},{56,0},{1,9},... | collective-permute-start | bytes 442376 | tf_op jit(solution)/shard_map/ppermute | solution.py:37
  18.6 7.1 %collective-permute-done.3 = bf16[384,192]{0,1:T(8,128)(2,1)S(1)} collective-permute-done((bf16[384,192]{0,1:T(8,128)(2,1)S(1)}, bf16[384,192]{0,1:T(8,128)(2,1)S(1)}, u32[]{:S(2)}, u32[]{:S(2)}) %collective-permute-start.3) | collective-permute-done | bytes 147488 | tf_op jit(solution)/shard_map/ppermute | solution.py:37
  25.9 3.3 %collective-permute-start.7 = (bf16[384,192]{0,1:T(8,128)(2,1)S(1)}, bf16[384,192]{0,1:T(8,128)(2,1)S(1)}, u32[]{:S(2)}, u32[]{:S(2)}) collective-permute-start(bf16[384,192]{0,1:T(8,128)(2,1)S(1)} %broadcast_select_fusion), channel_id=1, source_target_pairs={{0,56},{8,0},{16,8},{24,16},{32,24},{40,32},{48,40},{56,48},{1,57}... | collective-permute-start | bytes 442376 | tf_op jit(solution)/shard_map/ppermute | solution.py:41
  29.2 3.5 %collective-permute-done.4 = bf16[384,192]{0,1:T(8,128)(2,1)S(1)} collective-permute-done((bf16[384,192]{0,1:T(8,128)(2,1)S(1)}, bf16[384,192]{0,1:T(8,128)(2,1)S(1)}, u32[]{:S(2)}, u32[]{:S(2)}) %collective-permute-start.4) | collective-permute-done | bytes 147488 | tf_op jit(solution)/shard_map/ppermute | solution.py:37
  32.8 3.7 %collective-permute-start.8 = (bf16[384,192]{0,1:T(8,128)(2,1)S(1)}, bf16[384,192]{0,1:T(8,128)(2,1)S(1)}, u32[]{:S(2)}, u32[]{:S(2)}) collective-permute-start(bf16[384,192]{0,1:T(8,128)(2,1)S(1)} %collective-permute-done.7), channel_id=1, source_target_pairs={{0,56},{8,0},{16,8},{24,16},{32,24},{40,32},{48,40},{56,48},{1,57}... | collective-permute-start | bytes 442376 | tf_op jit(solution)/shard_map/ppermute | solution.py:41
  36.5 3.9 %collective-permute-done.5 = bf16[384,192]{0,1:T(8,128)(2,1)S(1)} collective-permute-done((bf16[384,192]{0,1:T(8,128)(2,1)S(1)}, bf16[384,192]{0,1:T(8,128)(2,1)S(1)}, u32[]{:S(2)}, u32[]{:S(2)}) %collective-permute-start.5) | collective-permute-done | bytes 147488 | tf_op jit(solution)/shard_map/ppermute | solution.py:37
  40.6 3.5 %collective-permute-start.9 = (bf16[384,192]{0,1:T(8,128)(2,1)S(1)}, bf16[384,192]{0,1:T(8,128)(2,1)S(1)}, u32[]{:S(2)}, u32[]{:S(2)}) collective-permute-start(bf16[384,192]{0,1:T(8,128)(2,1)S(1)} %collective-permute-done.8), channel_id=1, source_target_pairs={{0,56},{8,0},{16,8},{24,16},{32,24},{40,32},{48,40},{56,48},{1,57}... | collective-permute-start | bytes 442376 | tf_op jit(solution)/shard_map/ppermute | solution.py:41
  44.1 2.7 %collective-permute-done.6 = bf16[384,192]{0,1:T(8,128)(2,1)S(1)} collective-permute-done((bf16[384,192]{0,1:T(8,128)(2,1)S(1)}, bf16[384,192]{0,1:T(8,128)(2,1)S(1)}, u32[]{:S(2)}, u32[]{:S(2)}) %collective-permute-start.6) | collective-permute-done | bytes 147488 | tf_op jit(solution)/shard_map/ppermute | solution.py:37
  47.0 0.7 copy.39
  47.7 0.6 reshape_reshape.3
  48.6 0.6 gather_fusion.2
  49.2 0.6 gather_fusion.1
  49.9 9.7 %bitcast_convert_fusion = bf16[196,24,192]{0,2,1:T(8,128)(2,1)} fusion(bf16[10,128,192]{1,2,0:T(8,128)(2,1)S(1)} %gather_fusion.1, bf16[10,128,192]{1,2,0:T(8,128)(2,1)S(1)} %gather_fusion.2, bf16[1,1,10,24,128,128]{5,4,3,2,1,0:T(8,128)(2,1)} %param.4), kind=kOutput, calls=%fused_computation.9 | convolution fusion | flops 3828860928 | bytes 10653696 | tf_op jit(solution)/shard_map/tai,tarj->irj/dot_general | solution.py:70
  59.6 3.9 %copy.43 = bf16[196,24,192]{2,1,0:T(8,128)(2,1)S(1)} copy(bf16[196,24,192]{0,2,1:T(8,128)(2,1)} %bitcast_convert_fusion) | data formatting | bytes 3612672 | tf_op jit(solution)/shard_map/convert_element_type | solution.py:70
  63.5 3.2 %gather_fusion.3 = bf16[96,4,24,192]{3,2,1,0:T(8,128)(2,1)} fusion(bf16[49,4,24,192]{3,2,1,0:T(8,128)(2,1)S(1)} %bitcast.60, s32[1024]{0:T(1024)S(1)} %get-tuple-element.7), kind=kCustom, calls=%fused_computation.3 | custom fusion | bytes 7078272 | tf_op jit(solution)/shard_map/jit(_take)/gather | solution.py:76
  66.7 51.5 %all_to_all.18 = bf16[96,1,4,24,192]{4,3,2,1,0:T(8,128)(2,1)S(1)} all-to-all(bf16[96,1,4,24,192]{4,3,2,1,0:T(8,128)(2,1)} %bitcast.61), channel_id=1, replica_groups=mesh['grp'=4,'z'=8,'y'=4,'c'=2] {'grp'}, dimensions={0} | all-to-all | bytes 7077888 | tf_op jit(solution)/shard_map/all_to_all | solution.py:77
  118.1 2.6 %copy.45 = bf16[24,4,4,24,192]{4,3,2,1,0:T(8,128)(2,1)} copy(bf16[24,4,4,24,192]{4,3,2,0,1:T(8,128)(2,1)S(1)} %bitcast.62) | data formatting | bytes 7077888 | tf_op jit(solution)/shard_map/all_to_all | solution.py:77
  (36 shorter events, 1.3 us)
Async XLA Ops:
  0.0 18.6 %copy-start = (s32[48]{0:T(128)S(1)}, s32[48]{0:T(128)}, u32[]{:S(2)}) copy-start(s32[48]{0:T(128)} %param.7) | copy-start | bytes 580
  2.2 8.6 %collective-permute-start.2 = (bf16[96,192]{1,0:T(8,128)(2,1)S(1)}, bf16[96,192]{1,0:T(8,128)(2,1)S(1)}, u32[]{:S(2)}, u32[]{:S(2)}) collective-permute-start(bf16[96,192]{1,0:T(8,128)(2,1)S(1)} %all_gather.3), channel_id=1, source_target_pairs={{0,6},{2,0},{4,2},{6,4},{1,7},{3,1},{5,3},{7,5},{8,14},{10,8},{12,... | collective-permute-start | bytes 110600 | tf_op jit(solution)/shard_map/ppermute | solution.py:41
  5.2 5.3 %collective-permute-start = (bf16[96,192]{1,0:T(8,128)(2,1)S(1)}, bf16[96,192]{1,0:T(8,128)(2,1)S(1)}, u32[]{:S(2)}, u32[]{:S(2)}) collective-permute-start(bf16[96,192]{1,0:T(8,128)(2,1)S(1)} %all_gather.3), channel_id=1, source_target_pairs={{0,2},{2,4},{4,6},{6,0},{1,3},{3,5},{5,7},{7,1},{8,10},{10,12},{12... | collective-permute-start | bytes 110600 | tf_op jit(solution)/shard_map/ppermute | solution.py:37
  10.5 5.3 %collective-permute-start.1 = (bf16[96,192]{1,0:T(8,128)(2,1)S(1)}, bf16[96,192]{1,0:T(8,128)(2,1)S(1)}, u32[]{:S(2)}, u32[]{:S(2)}) collective-permute-start(bf16[96,192]{1,0:T(8,128)(2,1)S(1)} %collective-permute-done), channel_id=1, source_target_pairs={{0,2},{2,4},{4,6},{6,0},{1,3},{3,5},{5,7},{7,1},{8,10},{10,12},{12... | collective-permute-start | bytes 110600 | tf_op jit(solution)/shard_map/ppermute | solution.py:37
  16.6 9.1 %collective-permute-start.3 = (bf16[384,192]{0,1:T(8,128)(2,1)S(1)}, bf16[384,192]{0,1:T(8,128)(2,1)S(1)}, u32[]{:S(2)}, u32[]{:S(2)}) collective-permute-start(bf16[384,192]{0,1:T(8,128)(2,1)S(1)} %broadcast_select_fusion), channel_id=1, source_target_pairs={{0,8},{8,16},{16,24},{24,32},{32,40},{40,48},{48,56},{56,0},{1,9},... | collective-permute-start | bytes 442376 | tf_op jit(solution)/shard_map/ppermute | solution.py:37
  25.7 7.0 %collective-permute-start.4 = (bf16[384,192]{0,1:T(8,128)(2,1)S(1)}, bf16[384,192]{0,1:T(8,128)(2,1)S(1)}, u32[]{:S(2)}, u32[]{:S(2)}) collective-permute-start(bf16[384,192]{0,1:T(8,128)(2,1)S(1)} %collective-permute-done.3), channel_id=1, source_target_pairs={{0,8},{8,16},{16,24},{24,32},{32,40},{40,48},{48,56},{56,0},{1,9},... | collective-permute-start | bytes 442376 | tf_op jit(solution)/shard_map/ppermute | solution.py:37
  25.9 6.9 %collective-permute-start.7 = (bf16[384,192]{0,1:T(8,128)(2,1)S(1)}, bf16[384,192]{0,1:T(8,128)(2,1)S(1)}, u32[]{:S(2)}, u32[]{:S(2)}) collective-permute-start(bf16[384,192]{0,1:T(8,128)(2,1)S(1)} %broadcast_select_fusion), channel_id=1, source_target_pairs={{0,56},{8,0},{16,8},{24,16},{32,24},{40,32},{48,40},{56,48},{1,57}... | collective-permute-start | bytes 442376 | tf_op jit(solution)/shard_map/ppermute | solution.py:41
  32.7 7.7 %collective-permute-start.5 = (bf16[384,192]{0,1:T(8,128)(2,1)S(1)}, bf16[384,192]{0,1:T(8,128)(2,1)S(1)}, u32[]{:S(2)}, u32[]{:S(2)}) collective-permute-start(bf16[384,192]{0,1:T(8,128)(2,1)S(1)} %collective-permute-done.4), channel_id=1, source_target_pairs={{0,8},{8,16},{16,24},{24,32},{32,40},{40,48},{48,56},{56,0},{1,9},... | collective-permute-start | bytes 442376 | tf_op jit(solution)/shard_map/ppermute | solution.py:37
  32.8 7.8 %collective-permute-start.8 = (bf16[384,192]{0,1:T(8,128)(2,1)S(1)}, bf16[384,192]{0,1:T(8,128)(2,1)S(1)}, u32[]{:S(2)}, u32[]{:S(2)}) collective-permute-start(bf16[384,192]{0,1:T(8,128)(2,1)S(1)} %collective-permute-done.7), channel_id=1, source_target_pairs={{0,56},{8,0},{16,8},{24,16},{32,24},{40,32},{48,40},{56,48},{1,57}... | collective-permute-start | bytes 442376 | tf_op jit(solution)/shard_map/ppermute | solution.py:41
  40.4 6.4 %collective-permute-start.6 = (bf16[384,192]{0,1:T(8,128)(2,1)S(1)}, bf16[384,192]{0,1:T(8,128)(2,1)S(1)}, u32[]{:S(2)}, u32[]{:S(2)}) collective-permute-start(bf16[384,192]{0,1:T(8,128)(2,1)S(1)} %collective-permute-done.5), channel_id=1, source_target_pairs={{0,8},{8,16},{16,24},{24,32},{32,40},{40,48},{48,56},{56,0},{1,9},... | collective-permute-start | bytes 442376 | tf_op jit(solution)/shard_map/ppermute | solution.py:37
  40.6 6.4 %collective-permute-start.9 = (bf16[384,192]{0,1:T(8,128)(2,1)S(1)}, bf16[384,192]{0,1:T(8,128)(2,1)S(1)}, u32[]{:S(2)}, u32[]{:S(2)}) collective-permute-start(bf16[384,192]{0,1:T(8,128)(2,1)S(1)} %collective-permute-done.8), channel_id=1, source_target_pairs={{0,56},{8,0},{16,8},{24,16},{32,24},{40,32},{48,40},{56,48},{1,57}... | collective-permute-start | bytes 442376 | tf_op jit(solution)/shard_map/ppermute | solution.py:41

commit v4 on v3

--- a/solution.py
+++ b/solution.py
@@ -44,12 +44,17 @@
     return jnp.stack([got[o] for o in range(lo, lo + n)]), lo
 
 
+def direct(x, axis):
+    n = lax.axis_size(axis)
+    got = [x] + [lax.ppermute(x, axis, [(s, (s + o) % n) for s in range(n)]) for o in range(1, n)]
+    stack = jnp.stack(got)
+    want = (lax.axis_index(axis) - jnp.arange(n)) % n
+    return jnp.take(stack, want, axis=0, mode="clip")
+
+
 def gather_coef(coefficients):
     x = lax.all_gather(coefficients, "c", axis=0, tiled=True)
-    ny = lax.axis_size("y")
-    stack, lo = ring(x, "y")
-    want = (jnp.arange(ny) - lax.axis_index("y") - lo) % ny
-    x = jnp.take(stack, want, axis=0).reshape(-1, NMO)
+    x = direct(x, "y").reshape(-1, NMO)
     stack, lo = ring(x, "z")
     per = NSH // lax.axis_size("z")
     return stack.reshape(-1, NMO), per * (lax.axis_index("z") + lo)

time: 122 us -> 118 us (0.967)
  waiting for transfers between devices: 26 us -> 19 us
  starting transfers between devices: 15.6 us -> 16.9 us
    ppermute x6 -> x4, waiting for transfers between devices: 26 us -> 16.2 us  [ring(): f = lax.ppermute(f, axis, [(s, (s + 1) % n) for s in range(n)])]
    ppermute x0 -> x3, starting transfers between devices: none -> 4.67 us  [direct(): lax.ppermute(x, axis, [(s, (s + o) % n) for s in range(n)])]
    ppermute x4 -> x3, starting transfers between devices: 13.5 us -> 10.3 us  [ring(): b = lax.ppermute(b, axis, [(s, (s - 1) % n) for s in range(n)])]
    ppermute x0 -> x3, waiting for transfers between devices: none -> 2.88 us  [direct(): lax.ppermute(x, axis, [(s, (s + o) % n) for s in range(n)])]
  transfers between devices with their start and end apart: 10 -> 10, of which waited for: 7 -> 6; matrix products, arithmetic and copies ran while one was open for 2% -> 2% of each run, Pallas kernels for 0% -> 0%
where the time goes in v4:
time: 118 us; the launch traced here: 116 us
  blocking collectives  54.5 us (46%)
  waiting for transfers between devices  19 us (16%)
  starting transfers between devices  16.9 us (14%)
  local copies, waits for them, and re-layouts  13.6 us (12%)
  matrix products  9.68 us (8%)
  other arithmetic  1.86 us (2%)
    all_to_all x1, blocking collectives, body(): return lax.all_to_all(picked[:, None], 'grp', 0, 1, tiled=True)  52.3 us
    ppermute x4, waiting for transfers between devices, ring(): f = lax.ppermute(f, axis, [(s, (s + 1) % n) for s in range(n)])  16.2 us
    ppermute x3, starting transfers between devices, ring(): b = lax.ppermute(b, axis, [(s, (s - 1) % n) for s in range(n)])  10.3 us
    dot_general x1, matrix products, body(): jnp.einsum('tai,tarj->irj', la_coef, quarter, preferred_element_type=jnp....  9.68 us
    ppermute x3, starting transfers between devices, direct(): lax.ppermute(x, axis, [(s, (s + o) % n) for s in range(n)])  4.67 us
    convert_element_type x1, local copies, waits for them, and re-layouts, body(): jnp.einsum('tai,tarj->irj', la_coef, quarter, preferred_element_type=jnp....  3.87 us
    gather x1, local copies, waits for them, and re-layouts, body(): picked = jnp.take(pair_blocks, source, axis=0, mode='clip')  3.23 us
    ppermute x3, waiting for transfers between devices, direct(): lax.ppermute(x, axis, [(s, (s + o) % n) for s in range(n)])  2.88 us
  transfers between devices with their start and end apart: 10, of which 6 were waited for; matrix products, arithmetic and copies ran while one was open for 2% of the time, Pallas kernels for 0%

profile of v4, /device:TPU:2, one launch (start us, length us, event | category | flops | bytes accessed | tf_op | source)
XLA Modules:
  0.0 115.8 jit_solution(15238822254519482153)
XLA Ops:
  0.0 2.2 %all_gather.3 = bf16[96,192]{1,0:T(8,128)(2,1)S(1)} all-gather(bf16[48,192]{1,0:T(8,128)(2,1)} %param.5), channel_id=1, replica_groups=mesh['grp'=4,'z'=8,'y'=4,'c'=2] {'c'}, dimensions={0}, use_global_device_ids=true | all-gather | bytes 55296 | tf_op jit(solution)/shard_map/all_gather | solution.py:56
  2.2 3.1 %collective-permute-start.2 = (bf16[96,192]{1,0:T(8,128)(2,1)S(1)}, bf16[96,192]{1,0:T(8,128)(2,1)S(1)}, u32[]{:S(2)}, u32[]{:S(2)}) collective-permute-start(bf16[96,192]{1,0:T(8,128)(2,1)S(1)} %all_gather.3), channel_id=1, source_target_pairs={{0,6},{2,0},{4,2},{6,4},{1,7},{3,1},{5,3},{7,5},{8,14},{10,8},{12,... | collective-permute-start | bytes 110600 | tf_op jit(solution)/shard_map/ppermute | solution.py:49
  5.2 0.6 collective-permute-start.1
  5.9 1.0 collective-permute-start
  6.9 0.7 and_select_fusion
  7.6 0.9 convert_reduce_fusion
  8.5 2.4 %collective-permute-done.1 = bf16[96,192]{1,0:T(8,128)(2,1)S(1)} collective-permute-done((bf16[96,192]{1,0:T(8,128)(2,1)S(1)}, bf16[96,192]{1,0:T(8,128)(2,1)S(1)}, u32[]{:S(2)}, u32[]{:S(2)}) %collective-permute-start.1) | collective-permute-done | bytes 36896 | tf_op jit(solution)/shard_map/ppermute | solution.py:49
  12.1 2.0 %collective-permute-start.3 = (bf16[384,192]{0,1:T(8,128)(2,1)S(1)}, bf16[384,192]{0,1:T(8,128)(2,1)S(1)}, u32[]{:S(2)}, u32[]{:S(2)}) collective-permute-start(bf16[384,192]{0,1:T(8,128)(2,1)S(1)} %copy.47), channel_id=1, source_target_pairs={{0,8},{8,16},{16,24},{24,32},{32,40},{40,48},{48,56},{56,0},{1,9},... | collective-permute-start | bytes 442376 | tf_op jit(solution)/shard_map/ppermute | solution.py:37
  14.1 7.1 %collective-permute-done.3 = bf16[384,192]{0,1:T(8,128)(2,1)S(1)} collective-permute-done((bf16[384,192]{0,1:T(8,128)(2,1)S(1)}, bf16[384,192]{0,1:T(8,128)(2,1)S(1)}, u32[]{:S(2)}, u32[]{:S(2)}) %collective-permute-start.3) | collective-permute-done | bytes 147488 | tf_op jit(solution)/shard_map/ppermute | solution.py:37
  21.4 3.3 %collective-permute-start.7 = (bf16[384,192]{0,1:T(8,128)(2,1)S(1)}, bf16[384,192]{0,1:T(8,128)(2,1)S(1)}, u32[]{:S(2)}, u32[]{:S(2)}) collective-permute-start(bf16[384,192]{0,1:T(8,128)(2,1)S(1)} %copy.47), channel_id=1, source_target_pairs={{0,56},{8,0},{16,8},{24,16},{32,24},{40,32},{48,40},{56,48},{1,57}... | collective-permute-start | bytes 442376 | tf_op jit(solution)/shard_map/ppermute | solution.py:41
  24.7 2.9 %collective-permute-done.4 = bf16[384,192]{0,1:T(8,128)(2,1)S(1)} collective-permute-done((bf16[384,192]{0,1:T(8,128)(2,1)S(1)}, bf16[384,192]{0,1:T(8,128)(2,1)S(1)}, u32[]{:S(2)}, u32[]{:S(2)}) %collective-permute-start.4) | collective-permute-done | bytes 147488 | tf_op jit(solution)/shard_map/ppermute | solution.py:37
  27.5 3.5 %collective-permute-start.8 = (bf16[384,192]{0,1:T(8,128)(2,1)S(1)}, bf16[384,192]{0,1:T(8,128)(2,1)S(1)}, u32[]{:S(2)}, u32[]{:S(2)}) collective-permute-start(bf16[384,192]{0,1:T(8,128)(2,1)S(1)} %collective-permute-done.7), channel_id=1, source_target_pairs={{0,56},{8,0},{16,8},{24,16},{32,24},{40,32},{48,40},{56,48},{1,57}... | collective-permute-start | bytes 442376 | tf_op jit(solution)/shard_map/ppermute | solution.py:41
  31.0 3.5 %collective-permute-done.5 = bf16[384,192]{0,1:T(8,128)(2,1)S(1)} collective-permute-done((bf16[384,192]{0,1:T(8,128)(2,1)S(1)}, bf16[384,192]{0,1:T(8,128)(2,1)S(1)}, u32[]{:S(2)}, u32[]{:S(2)}) %collective-permute-start.5) | collective-permute-done | bytes 147488 | tf_op jit(solution)/shard_map/ppermute | solution.py:37
  34.8 3.5 %collective-permute-start.9 = (bf16[384,192]{0,1:T(8,128)(2,1)S(1)}, bf16[384,192]{0,1:T(8,128)(2,1)S(1)}, u32[]{:S(2)}, u32[]{:S(2)}) collective-permute-start(bf16[384,192]{0,1:T(8,128)(2,1)S(1)} %collective-permute-done.8), channel_id=1, source_target_pairs={{0,56},{8,0},{16,8},{24,16},{32,24},{40,32},{48,40},{56,48},{1,57}... | collective-permute-start | bytes 442376 | tf_op jit(solution)/shard_map/ppermute | solution.py:41
  38.2 2.7 %collective-permute-done.6 = bf16[384,192]{0,1:T(8,128)(2,1)S(1)} collective-permute-done((bf16[384,192]{0,1:T(8,128)(2,1)S(1)}, bf16[384,192]{0,1:T(8,128)(2,1)S(1)}, u32[]{:S(2)}, u32[]{:S(2)}) %collective-permute-start.6) | collective-permute-done | bytes 147488 | tf_op jit(solution)/shard_map/ppermute | solution.py:37
  41.2 0.7 copy.39
  41.9 0.6 reshape_reshape.3
  42.7 0.6 gather_fusion.2
  43.4 0.6 gather_fusion.1
  44.0 9.7 %bitcast_convert_fusion = bf16[196,24,192]{0,2,1:T(8,128)(2,1)} fusion(bf16[10,128,192]{1,2,0:T(8,128)(2,1)S(1)} %gather_fusion.1, bf16[10,128,192]{1,2,0:T(8,128)(2,1)S(1)} %gather_fusion.2, bf16[1,1,10,24,128,128]{5,4,3,2,1,0:T(8,128)(2,1)} %param.4), kind=kOutput, calls=%fused_computation.9 | convolution fusion | flops 3828860928 | bytes 10653696 | tf_op jit(solution)/shard_map/tai,tarj->irj/dot_general | solution.py:75
  53.7 3.9 %copy.43 = bf16[196,24,192]{2,1,0:T(8,128)(2,1)S(1)} copy(bf16[196,24,192]{0,2,1:T(8,128)(2,1)} %bitcast_convert_fusion) | data formatting | bytes 3612672 | tf_op jit(solution)/shard_map/convert_element_type | solution.py:75
  57.6 3.2 %gather_fusion.3 = bf16[96,4,24,192]{3,2,1,0:T(8,128)(2,1)} fusion(bf16[49,4,24,192]{3,2,1,0:T(8,128)(2,1)S(1)} %bitcast.60, s32[1024]{0:T(1024)S(1)} %get-tuple-element.7), kind=kCustom, calls=%fused_computation.3 | custom fusion | bytes 7078272 | tf_op jit(solution)/shard_map/jit(_take)/gather | solution.py:81
  60.8 52.3 %all_to_all.18 = bf16[96,1,4,24,192]{4,3,2,1,0:T(8,128)(2,1)S(1)} all-to-all(bf16[96,1,4,24,192]{4,3,2,1,0:T(8,128)(2,1)} %bitcast.61), channel_id=1, replica_groups=mesh['grp'=4,'z'=8,'y'=4,'c'=2] {'grp'}, dimensions={0} | all-to-all | bytes 7077888 | tf_op jit(solution)/shard_map/all_to_all | solution.py:82
  113.2 2.6 %copy.45 = bf16[24,4,4,24,192]{4,3,2,1,0:T(8,128)(2,1)} copy(bf16[24,4,4,24,192]{4,3,2,0,1:T(8,128)(2,1)S(1)} %bitcast.62) | data formatting | bytes 7077888 | tf_op jit(solution)/shard_map/all_to_all | solution.py:82
  (32 shorter events, 2.1 us)
Async XLA Ops:
  0.0 14.1 %copy-start = (s32[48]{0:T(128)S(1)}, s32[48]{0:T(128)}, u32[]{:S(2)}) copy-start(s32[48]{0:T(128)} %param.7) | copy-start | bytes 580
  2.2 6.3 %collective-permute-start.2 = (bf16[96,192]{1,0:T(8,128)(2,1)S(1)}, bf16[96,192]{1,0:T(8,128)(2,1)S(1)}, u32[]{:S(2)}, u32[]{:S(2)}) collective-permute-start(bf16[96,192]{1,0:T(8,128)(2,1)S(1)} %all_gather.3), channel_id=1, source_target_pairs={{0,6},{2,0},{4,2},{6,4},{1,7},{3,1},{5,3},{7,5},{8,14},{10,8},{12,... | collective-permute-start | bytes 110600 | tf_op jit(solution)/shard_map/ppermute | solution.py:49
  5.2 5.6 %collective-permute-start.1 = (bf16[96,192]{1,0:T(8,128)(2,1)S(1)}, bf16[96,192]{1,0:T(8,128)(2,1)S(1)}, u32[]{:S(2)}, u32[]{:S(2)}) collective-permute-start(bf16[96,192]{1,0:T(8,128)(2,1)S(1)} %all_gather.3), channel_id=1, source_target_pairs={{0,4},{2,6},{4,0},{6,2},{1,5},{3,7},{5,1},{7,3},{8,12},{10,14},{12... | collective-permute-start | bytes 110600 | tf_op jit(solution)/shard_map/ppermute | solution.py:49
  5.9 5.5 %collective-permute-start = (bf16[96,192]{1,0:T(8,128)(2,1)S(1)}, bf16[96,192]{1,0:T(8,128)(2,1)S(1)}, u32[]{:S(2)}, u32[]{:S(2)}) collective-permute-start(bf16[96,192]{1,0:T(8,128)(2,1)S(1)} %all_gather.3), channel_id=1, source_target_pairs={{0,2},{2,4},{4,6},{6,0},{1,3},{3,5},{5,7},{7,1},{8,10},{10,12},{12... | collective-permute-start | bytes 110600 | tf_op jit(solution)/shard_map/ppermute | solution.py:49
  12.1 9.1 %collective-permute-start.3 = (bf16[384,192]{0,1:T(8,128)(2,1)S(1)}, bf16[384,192]{0,1:T(8,128)(2,1)S(1)}, u32[]{:S(2)}, u32[]{:S(2)}) collective-permute-start(bf16[384,192]{0,1:T(8,128)(2,1)S(1)} %copy.47), channel_id=1, source_target_pairs={{0,8},{8,16},{16,24},{24,32},{32,40},{40,48},{48,56},{56,0},{1,9},... | collective-permute-start | bytes 442376 | tf_op jit(solution)/shard_map/ppermute | solution.py:37
  21.2 6.4 %collective-permute-start.4 = (bf16[384,192]{0,1:T(8,128)(2,1)S(1)}, bf16[384,192]{0,1:T(8,128)(2,1)S(1)}, u32[]{:S(2)}, u32[]{:S(2)}) collective-permute-start(bf16[384,192]{0,1:T(8,128)(2,1)S(1)} %collective-permute-done.3), channel_id=1, source_target_pairs={{0,8},{8,16},{16,24},{24,32},{32,40},{40,48},{48,56},{56,0},{1,9},... | collective-permute-start | bytes 442376 | tf_op jit(solution)/shard_map/ppermute | solution.py:37
  21.4 6.2 %collective-permute-start.7 = (bf16[384,192]{0,1:T(8,128)(2,1)S(1)}, bf16[384,192]{0,1:T(8,128)(2,1)S(1)}, u32[]{:S(2)}, u32[]{:S(2)}) collective-permute-start(bf16[384,192]{0,1:T(8,128)(2,1)S(1)} %copy.47), channel_id=1, source_target_pairs={{0,56},{8,0},{16,8},{24,16},{32,24},{40,32},{48,40},{56,48},{1,57}... | collective-permute-start | bytes 442376 | tf_op jit(solution)/shard_map/ppermute | solution.py:41
  27.5 7.0 %collective-permute-start.5 = (bf16[384,192]{0,1:T(8,128)(2,1)S(1)}, bf16[384,192]{0,1:T(8,128)(2,1)S(1)}, u32[]{:S(2)}, u32[]{:S(2)}) collective-permute-start(bf16[384,192]{0,1:T(8,128)(2,1)S(1)} %collective-permute-done.4), channel_id=1, source_target_pairs={{0,8},{8,16},{16,24},{24,32},{32,40},{40,48},{48,56},{56,0},{1,9},... | collective-permute-start | bytes 442376 | tf_op jit(solution)/shard_map/ppermute | solution.py:37
  27.5 7.2 %collective-permute-start.8 = (bf16[384,192]{0,1:T(8,128)(2,1)S(1)}, bf16[384,192]{0,1:T(8,128)(2,1)S(1)}, u32[]{:S(2)}, u32[]{:S(2)}) collective-permute-start(bf16[384,192]{0,1:T(8,128)(2,1)S(1)} %collective-permute-done.7), channel_id=1, source_target_pairs={{0,56},{8,0},{16,8},{24,16},{32,24},{40,32},{48,40},{56,48},{1,57}... | collective-permute-start | bytes 442376 | tf_op jit(solution)/shard_map/ppermute | solution.py:41
  34.6 6.4 %collective-permute-start.6 = (bf16[384,192]{0,1:T(8,128)(2,1)S(1)}, bf16[384,192]{0,1:T(8,128)(2,1)S(1)}, u32[]{:S(2)}, u32[]{:S(2)}) collective-permute-start(bf16[384,192]{0,1:T(8,128)(2,1)S(1)} %collective-permute-done.5), channel_id=1, source_target_pairs={{0,8},{8,16},{16,24},{24,32},{32,40},{40,48},{48,56},{56,0},{1,9},... | collective-permute-start | bytes 442376 | tf_op jit(solution)/shard_map/ppermute | solution.py:37
  34.8 6.4 %collective-permute-start.9 = (bf16[384,192]{0,1:T(8,128)(2,1)S(1)}, bf16[384,192]{0,1:T(8,128)(2,1)S(1)}, u32[]{:S(2)}, u32[]{:S(2)}) collective-permute-start(bf16[384,192]{0,1:T(8,128)(2,1)S(1)} %collective-permute-done.8), channel_id=1, source_target_pairs={{0,56},{8,0},{16,8},{24,16},{32,24},{40,32},{48,40},{56,48},{1,57}... | collective-permute-start | bytes 442376 | tf_op jit(solution)/shard_map/ppermute | solution.py:41

commit v5 on v4

--- a/solution.py
+++ b/solution.py
@@ -52,12 +52,36 @@
     return jnp.take(stack, want, axis=0, mode="clip")
 
 
+def zring8(x):
+    nz = lax.axis_size("z")
+    zc = ("z", "c")
+
+    def at(z, c):
+        return (z % nz) * 2 + c
+
+    f1 = lax.ppermute(x, zc, [(at(z, 0), at(z + 1, 0)) for z in range(nz)] + [(at(z, 1), at(z + 2, 1)) for z in range(nz)])
+    b1 = lax.ppermute(x, zc, [(at(z, 0), at(z - 1, 0)) for z in range(nz)] + [(at(z, 1), at(z - 2, 1)) for z in range(nz)])
+    pa = lax.ppermute(f1, zc, [(at(z, 1), at(z + 1, 0)) for z in range(nz)])
+    pb = lax.ppermute(f1, zc, [(at(z, 1), at(z + 2, 1)) for z in range(nz)])
+    pc = lax.ppermute(b1, zc, [(at(z, 1), at(z - 1, 0)) for z in range(nz)])
+    first = lax.axis_index("c") == 0
+    mine = jnp.stack([f1, b1, jnp.where(first, pa, pb), pc])
+    theirs = lax.ppermute(mine, "c", [(0, 1), (1, 0)])
+    a = jnp.where(first, mine, theirs)
+    b = jnp.where(first, theirs, mine)
+    return jnp.concatenate([b[2], a[2], b[0], a[0], x, a[1], b[1], a[3]], axis=0), -4
+
+
 def gather_coef(coefficients):
     x = lax.all_gather(coefficients, "c", axis=0, tiled=True)
     x = direct(x, "y").reshape(-1, NMO)
-    stack, lo = ring(x, "z")
+    if lax.axis_size("z") == 8:
+        rows, lo = zring8(x)
+    else:
+        stack, lo = ring(x, "z")
+        rows = stack.reshape(-1, NMO)
     per = NSH // lax.axis_size("z")
-    return stack.reshape(-1, NMO), per * (lax.axis_index("z") + lo)
+    return rows, per * (lax.axis_index("z") + lo)
 
 
 def body(integrals, coefficients, tile_blocks, block_owner):

time: 118 us -> 116 us (0.983)
  the two profiles are of different devices: /device:TPU:2 before, /device:TPU:32 now
where the time goes in v5:
time: 116 us; the launch traced here: 115 us
  blocking collectives  61.2 us (53%)
  waiting for transfers between devices  20.5 us (18%)
  local copies, waits for them, and re-layouts  12.3 us (11%)
  starting transfers between devices  10.2 us (9%)
  matrix products  9.67 us (8%)
  other arithmetic  1.42 us (1%)
    all_to_all x1, blocking collectives, body(): return lax.all_to_all(picked[:, None], 'grp', 0, 1, tiled=True)  59 us
    dot_general x1, matrix products, body(): jnp.einsum('tai,tarj->irj', la_coef, quarter, preferred_element_type=jnp....  9.67 us
    ppermute x1, waiting for transfers between devices, zring8(): pa = lax.ppermute(f1, zc, [(at(z, 1), at(z + 1, 0)) for z in range(nz)])  6.52 us
    ppermute x3, starting transfers between devices, direct(): lax.ppermute(x, axis, [(s, (s + o) % n) for s in range(n)])  4.67 us
    ppermute x1, waiting for transfers between devices, zring8(): lax.ppermute(x, zc, [(at(z, 0), at(z + 1, 0)) for z in range(nz)] + [(at(...  4.06 us
    convert_element_type x1, local copies, waits for them, and re-layouts, body(): jnp.einsum('tai,tarj->irj', la_coef, quarter, preferred_element_type=jnp....  3.87 us
    ppermute x3, waiting for transfers between devices, direct(): lax.ppermute(x, axis, [(s, (s + o) % n) for s in range(n)])  3.8 us
    gather x1, local copies, waits for them, and re-layouts, body(): picked = jnp.take(pair_blocks, source, axis=0, mode='clip')  3.23 us
  transfers between devices with their start and end apart: 9, of which 7 were waited for; matrix products, arithmetic and copies ran while one was open for 1% of the time, Pallas kernels for 0%

profile of v5, /device:TPU:32, one launch (start us, length us, event | category | flops | bytes accessed | tf_op | source)
XLA Modules:
  0.0 115.4 jit_solution(8607662560070958432)
XLA Ops:
  0.0 2.2 %all_gather.3 = bf16[96,192]{1,0:T(8,128)(2,1)S(1)} all-gather(bf16[48,192]{1,0:T(8,128)(2,1)} %param.5), channel_id=1, replica_groups=mesh['grp'=4,'z'=8,'y'=4,'c'=2] {'c'}, dimensions={0}, use_global_device_ids=true | all-gather | bytes 55296 | tf_op jit(solution)/shard_map/all_gather | solution.py:76
  2.2 3.1 %collective-permute-start.2 = (bf16[96,192]{1,0:T(8,128)(2,1)S(1)}, bf16[96,192]{1,0:T(8,128)(2,1)S(1)}, u32[]{:S(2)}, u32[]{:S(2)}) collective-permute-start(bf16[96,192]{1,0:T(8,128)(2,1)S(1)} %all_gather.3), channel_id=1, source_target_pairs={{0,6},{2,0},{4,2},{6,4},{1,7},{3,1},{5,3},{7,5},{8,14},{10,8},{12,... | collective-permute-start | bytes 110600 | tf_op jit(solution)/shard_map/ppermute | solution.py:49
  5.2 0.6 collective-permute-start.1
  5.9 1.0 collective-permute-start
  6.9 0.7 and_select_fusion
  7.6 3.3 %collective-permute-done.1 = bf16[96,192]{1,0:T(8,128)(2,1)S(1)} collective-permute-done((bf16[96,192]{1,0:T(8,128)(2,1)S(1)}, bf16[96,192]{1,0:T(8,128)(2,1)S(1)}, u32[]{:S(2)}, u32[]{:S(2)}) %collective-permute-start.1) | collective-permute-done | bytes 36896 | tf_op jit(solution)/shard_map/ppermute | solution.py:49
  10.8 0.5 collective-permute-done
  11.4 0.6 gather_fusion
  12.1 2.0 %collective-permute-start.3 = (bf16[384,192]{0,1:T(8,128)(2,1)S(1)}, bf16[384,192]{0,1:T(8,128)(2,1)S(1)}, u32[]{:S(2)}, u32[]{:S(2)}) collective-permute-start(bf16[384,192]{0,1:T(8,128)(2,1)S(1)} %copy.32), channel_id=1, source_target_pairs={{0,8},{8,16},{16,24},{24,32},{32,40},{40,48},{48,56},{56,0},{1,17}... | collective-permute-start | bytes 442376 | tf_op jit(solution)/shard_map/ppermute | solution.py:62
  14.5 4.1 %collective-permute-done.3 = bf16[384,192]{0,1:T(8,128)(2,1)S(1)} collective-permute-done((bf16[384,192]{0,1:T(8,128)(2,1)S(1)}, bf16[384,192]{0,1:T(8,128)(2,1)S(1)}, u32[]{:S(2)}, u32[]{:S(2)}) %collective-permute-start.3) | collective-permute-done | bytes 147488 | tf_op jit(solution)/shard_map/ppermute | solution.py:62
  18.5 0.7 collective-permute-start.6
  19.2 1.3 %collective-permute-start.5 = (bf16[384,192]{0,1:T(8,128)(2,1)S(1)}, bf16[384,192]{0,1:T(8,128)(2,1)S(1)}, u32[]{:S(2)}, u32[]{:S(2)}) collective-permute-start(bf16[384,192]{0,1:T(8,128)(2,1)S(1)} %collective-permute-done.3), channel_id=1, source_target_pairs={{1,8},{9,16},{17,24},{25,32},{33,40},{41,48},{49,56},{57,0},{3,10}... | collective-permute-start | bytes 442376 | tf_op jit(solution)/shard_map/ppermute | solution.py:64
  20.5 2.0 %collective-permute-done.4 = bf16[384,192]{0,1:T(8,128)(2,1)S(1)} collective-permute-done((bf16[384,192]{0,1:T(8,128)(2,1)S(1)}, bf16[384,192]{0,1:T(8,128)(2,1)S(1)}, u32[]{:S(2)}, u32[]{:S(2)}) %collective-permute-start.4) | collective-permute-done | bytes 147488 | tf_op jit(solution)/shard_map/ppermute | solution.py:63
  22.5 1.3 %collective-permute-start.7 = (bf16[384,192]{0,1:T(8,128)(2,1)S(1)}, bf16[384,192]{0,1:T(8,128)(2,1)S(1)}, u32[]{:S(2)}, u32[]{:S(2)}) collective-permute-start(bf16[384,192]{0,1:T(8,128)(2,1)S(1)} %collective-permute-done.4), channel_id=1, source_target_pairs={{1,56},{9,0},{17,8},{25,16},{33,24},{41,32},{49,40},{57,48},{3,58}... | collective-permute-start | bytes 442376 | tf_op jit(solution)/shard_map/ppermute | solution.py:66
  23.8 6.5 %collective-permute-done.5 = bf16[384,192]{0,1:T(8,128)(2,1)S(1)} collective-permute-done((bf16[384,192]{0,1:T(8,128)(2,1)S(1)}, bf16[384,192]{0,1:T(8,128)(2,1)S(1)}, u32[]{:S(2)}, u32[]{:S(2)}) %collective-permute-start.5) | collective-permute-done | bytes 147488 | tf_op jit(solution)/shard_map/ppermute | solution.py:64
  30.4 2.3 %collective-permute-done.7 = bf16[384,192]{0,1:T(8,128)(2,1)S(1)} collective-permute-done((bf16[384,192]{0,1:T(8,128)(2,1)S(1)}, bf16[384,192]{0,1:T(8,128)(2,1)S(1)}, u32[]{:S(2)}, u32[]{:S(2)}) %collective-permute-start.7) | collective-permute-done | bytes 147488 | tf_op jit(solution)/shard_map/ppermute | solution.py:66
  33.1 1.8 %collective-permute-done.8 = bf16[4,384,192]{1,2,0:T(8,128)(2,1)S(1)} collective-permute-done((bf16[4,384,192]{1,2,0:T(8,128)(2,1)S(1)}, bf16[4,384,192]{1,2,0:T(8,128)(2,1)S(1)}, u32[]{:S(2)}, u32[]{:S(2)}) %collective-permute-start.8) | collective-permute-done | bytes 589856 | tf_op jit(solution)/shard_map/ppermute | solution.py:69
  35.7 0.6 gather_fusion.2
  36.3 0.6 gather_fusion.1
  37.0 9.7 %bitcast_convert_fusion = bf16[196,24,192]{0,2,1:T(8,128)(2,1)} fusion(bf16[10,128,192]{1,2,0:T(8,128)(2,1)S(1)} %gather_fusion.1, bf16[10,128,192]{1,2,0:T(8,128)(2,1)S(1)} %gather_fusion.2, bf16[1,1,10,24,128,128]{5,4,3,2,1,0:T(8,128)(2,1)} %param.4), kind=kOutput, calls=%fused_computation.9 | convolution fusion | flops 3828860928 | bytes 10653696 | tf_op jit(solution)/shard_map/tai,tarj->irj/dot_general | solution.py:99
  46.6 3.9 %copy.38 = bf16[196,24,192]{2,1,0:T(8,128)(2,1)S(1)} copy(bf16[196,24,192]{0,2,1:T(8,128)(2,1)} %bitcast_convert_fusion) | data formatting | bytes 3612672 | tf_op jit(solution)/shard_map/convert_element_type | solution.py:99
  50.5 3.2 %gather_fusion.3 = bf16[96,4,24,192]{3,2,1,0:T(8,128)(2,1)} fusion(bf16[49,4,24,192]{3,2,1,0:T(8,128)(2,1)S(1)} %bitcast.81, s32[1024]{0:T(1024)S(1)} %get-tuple-element.9), kind=kCustom, calls=%fused_computation.3 | custom fusion | bytes 7078272 | tf_op jit(solution)/shard_map/jit(_take)/gather | solution.py:105
  53.7 59.0 %all_to_all.18 = bf16[96,1,4,24,192]{4,3,2,1,0:T(8,128)(2,1)S(1)} all-to-all(bf16[96,1,4,24,192]{4,3,2,1,0:T(8,128)(2,1)} %bitcast.82), channel_id=1, replica_groups=mesh['grp'=4,'z'=8,'y'=4,'c'=2] {'grp'}, dimensions={0} | all-to-all | bytes 7077888 | tf_op jit(solution)/shard_map/all_to_all | solution.py:106
  112.8 2.6 %copy.40 = bf16[24,4,4,24,192]{4,3,2,1,0:T(8,128)(2,1)} copy(bf16[24,4,4,24,192]{4,3,2,0,1:T(8,128)(2,1)S(1)} %bitcast.83) | data formatting | bytes 7077888 | tf_op jit(solution)/shard_map/all_to_all | solution.py:106
  (30 shorter events, 1.7 us)
Async XLA Ops:
  0.0 14.1 %copy-start = (s32[48]{0:T(128)S(1)}, s32[48]{0:T(128)}, u32[]{:S(2)}) copy-start(s32[48]{0:T(128)} %param.7) | copy-start | bytes 580
  2.2 5.4 %collective-permute-start.2 = (bf16[96,192]{1,0:T(8,128)(2,1)S(1)}, bf16[96,192]{1,0:T(8,128)(2,1)S(1)}, u32[]{:S(2)}, u32[]{:S(2)}) collective-permute-start(bf16[96,192]{1,0:T(8,128)(2,1)S(1)} %all_gather.3), channel_id=1, source_target_pairs={{0,6},{2,0},{4,2},{6,4},{1,7},{3,1},{5,3},{7,5},{8,14},{10,8},{12,... | collective-permute-start | bytes 110600 | tf_op jit(solution)/shard_map/ppermute | solution.py:49
  5.2 5.6 %collective-permute-start.1 = (bf16[96,192]{1,0:T(8,128)(2,1)S(1)}, bf16[96,192]{1,0:T(8,128)(2,1)S(1)}, u32[]{:S(2)}, u32[]{:S(2)}) collective-permute-start(bf16[96,192]{1,0:T(8,128)(2,1)S(1)} %all_gather.3), channel_id=1, source_target_pairs={{0,4},{2,6},{4,0},{6,2},{1,5},{3,7},{5,1},{7,3},{8,12},{10,14},{12... | collective-permute-start | bytes 110600 | tf_op jit(solution)/shard_map/ppermute | solution.py:49
  5.9 5.5 %collective-permute-start = (bf16[96,192]{1,0:T(8,128)(2,1)S(1)}, bf16[96,192]{1,0:T(8,128)(2,1)S(1)}, u32[]{:S(2)}, u32[]{:S(2)}) collective-permute-start(bf16[96,192]{1,0:T(8,128)(2,1)S(1)} %all_gather.3), channel_id=1, source_target_pairs={{0,2},{2,4},{4,6},{6,0},{1,3},{3,5},{5,7},{7,1},{8,10},{10,12},{12... | collective-permute-start | bytes 110600 | tf_op jit(solution)/shard_map/ppermute | solution.py:49
  12.1 6.4 %collective-permute-start.3 = (bf16[384,192]{0,1:T(8,128)(2,1)S(1)}, bf16[384,192]{0,1:T(8,128)(2,1)S(1)}, u32[]{:S(2)}, u32[]{:S(2)}) collective-permute-start(bf16[384,192]{0,1:T(8,128)(2,1)S(1)} %copy.32), channel_id=1, source_target_pairs={{0,8},{8,16},{16,24},{24,32},{32,40},{40,48},{48,56},{56,0},{1,17}... | collective-permute-start | bytes 442376 | tf_op jit(solution)/shard_map/ppermute | solution.py:62
  14.3 8.2 %collective-permute-start.4 = (bf16[384,192]{0,1:T(8,128)(2,1)S(1)}, bf16[384,192]{0,1:T(8,128)(2,1)S(1)}, u32[]{:S(2)}, u32[]{:S(2)}) collective-permute-start(bf16[384,192]{0,1:T(8,128)(2,1)S(1)} %copy.32), channel_id=1, source_target_pairs={{0,56},{8,0},{16,8},{24,16},{32,24},{40,32},{48,40},{56,48},{1,49}... | collective-permute-start | bytes 442376 | tf_op jit(solution)/shard_map/ppermute | solution.py:63
  18.5 5.3 %collective-permute-start.6 = (bf16[384,192]{0,1:T(8,128)(2,1)S(1)}, bf16[384,192]{0,1:T(8,128)(2,1)S(1)}, u32[]{:S(2)}, u32[]{:S(2)}) collective-permute-start(bf16[384,192]{0,1:T(8,128)(2,1)S(1)} %collective-permute-done.3), channel_id=1, source_target_pairs={{1,17},{9,25},{17,33},{25,41},{33,49},{41,57},{49,1},{57,9},{3,19}... | collective-permute-start | bytes 442376 | tf_op jit(solution)/shard_map/ppermute | solution.py:65
  19.2 11.1 %collective-permute-start.5 = (bf16[384,192]{0,1:T(8,128)(2,1)S(1)}, bf16[384,192]{0,1:T(8,128)(2,1)S(1)}, u32[]{:S(2)}, u32[]{:S(2)}) collective-permute-start(bf16[384,192]{0,1:T(8,128)(2,1)S(1)} %collective-permute-done.3), channel_id=1, source_target_pairs={{1,8},{9,16},{17,24},{25,32},{33,40},{41,48},{49,56},{57,0},{3,10}... | collective-permute-start | bytes 442376 | tf_op jit(solution)/shard_map/ppermute | solution.py:64
  22.5 10.2 %collective-permute-start.7 = (bf16[384,192]{0,1:T(8,128)(2,1)S(1)}, bf16[384,192]{0,1:T(8,128)(2,1)S(1)}, u32[]{:S(2)}, u32[]{:S(2)}) collective-permute-start(bf16[384,192]{0,1:T(8,128)(2,1)S(1)} %collective-permute-done.4), channel_id=1, source_target_pairs={{1,56},{9,0},{17,8},{25,16},{33,24},{41,32},{49,40},{57,48},{3,58}... | collective-permute-start | bytes 442376 | tf_op jit(solution)/shard_map/ppermute | solution.py:66
  32.8 2.1 %collective-permute-start.8 = (bf16[4,384,192]{1,2,0:T(8,128)(2,1)S(1)}, bf16[4,384,192]{1,2,0:T(8,128)(2,1)S(1)}, u32[]{:S(2)}, u32[]{:S(2)}) collective-permute-start(bf16[4,384,192]{1,2,0:T(8,128)(2,1)S(1)} %pad_maximum_fusion), channel_id=1, source_target_pairs={{0,1},{1,0},{2,3},{3,2},{4,5},{5,4},{6,7},{7,6},{8,9},{9,8},{10,11... | collective-permute-start | bytes 1769480 | tf_op jit(solution)/shard_map/ppermute | solution.py:69

commit v6 on v5

--- a/solution.py
+++ b/solution.py
@@ -62,7 +62,11 @@
     f1 = lax.ppermute(x, zc, [(at(z, 0), at(z + 1, 0)) for z in range(nz)] + [(at(z, 1), at(z + 2, 1)) for z in range(nz)])
     b1 = lax.ppermute(x, zc, [(at(z, 0), at(z - 1, 0)) for z in range(nz)] + [(at(z, 1), at(z - 2, 1)) for z in range(nz)])
     pa = lax.ppermute(f1, zc, [(at(z, 1), at(z + 1, 0)) for z in range(nz)])
-    pb = lax.ppermute(f1, zc, [(at(z, 1), at(z + 2, 1)) for z in range(nz)])
+    cut = x.shape[0] // 2
+    pb = jnp.concatenate([
+        lax.ppermute(f1[:cut], zc, [(at(z, 1), at(z + 2, 1)) for z in range(nz)]),
+        lax.ppermute(b1[cut:], zc, [(at(z, 1), at(z - 2, 1)) for z in range(nz)]),
+    ], axis=0)
     pc = lax.ppermute(b1, zc, [(at(z, 1), at(z - 1, 0)) for z in range(nz)])
     first = lax.axis_index("c") == 0
     mine = jnp.stack([f1, b1, jnp.where(first, pa, pb), pc])

time: 116 us -> 118 us (1.017)
  the two profiles are of different devices: /device:TPU:32 before, /device:TPU:2 now
where the time goes in v6:
time: 118 us; the launch traced here: 117 us
  blocking collectives  60.5 us (51%)
  waiting for transfers between devices  17.1 us (14%)
  starting transfers between devices  15.5 us (13%)
  local copies, waits for them, and re-layouts  12.4 us (11%)
  matrix products  9.68 us (8%)
  other arithmetic  1.5 us (1%)
    all_to_all x1, blocking collectives, body(): return lax.all_to_all(picked[:, None], 'grp', 0, 1, tiled=True)  58.3 us
    dot_general x1, matrix products, body(): jnp.einsum('tai,tarj->irj', la_coef, quarter, preferred_element_type=jnp....  9.68 us
    ppermute x1, starting transfers between devices, zring8(): lax.ppermute(x, zc, [(at(z, 0), at(z - 1, 0)) for z in range(nz)] + [(at(...  5.93 us
    ppermute x1, waiting for transfers between devices, zring8(): pa = lax.ppermute(f1, zc, [(at(z, 1), at(z + 1, 0)) for z in range(nz)])  5.03 us
    ppermute x3, starting transfers between devices, direct(): lax.ppermute(x, axis, [(s, (s + o) % n) for s in range(n)])  4.67 us
    convert_element_type x1, local copies, waits for them, and re-layouts, body(): jnp.einsum('tai,tarj->irj', la_coef, quarter, preferred_element_type=jnp....  3.87 us
    ppermute x3, waiting for transfers between devices, direct(): lax.ppermute(x, axis, [(s, (s + o) % n) for s in range(n)])  3.8 us
    ppermute x1, waiting for transfers between devices, zring8(): lax.ppermute(x, zc, [(at(z, 0), at(z - 1, 0)) for z in range(nz)] + [(at(...  3.78 us
  transfers between devices with their start and end apart: 10, of which 6 were waited for; matrix products, arithmetic and copies ran while one was open for 1% of the time, Pallas kernels for 0%

profile of v6, /device:TPU:2, one launch (start us, length us, event | category | flops | bytes accessed | tf_op | source)
XLA Modules:
  0.0 116.9 jit_solution(3841749780648894499)
XLA Ops:
  0.0 2.2 %all_gather.3 = bf16[96,192]{1,0:T(8,128)(2,1)S(1)} all-gather(bf16[48,192]{1,0:T(8,128)(2,1)} %param.5), channel_id=1, replica_groups=mesh['grp'=4,'z'=8,'y'=4,'c'=2] {'c'}, dimensions={0}, use_global_device_ids=true | all-gather | bytes 55296 | tf_op jit(solution)/shard_map/all_gather | solution.py:80
  2.2 3.1 %collective-permute-start.2 = (bf16[96,192]{1,0:T(8,128)(2,1)S(1)}, bf16[96,192]{1,0:T(8,128)(2,1)S(1)}, u32[]{:S(2)}, u32[]{:S(2)}) collective-permute-start(bf16[96,192]{1,0:T(8,128)(2,1)S(1)} %all_gather.3), channel_id=1, source_target_pairs={{0,6},{2,0},{4,2},{6,4},{1,7},{3,1},{5,3},{7,5},{8,14},{10,8},{12,... | collective-permute-start | bytes 110600 | tf_op jit(solution)/shard_map/ppermute | solution.py:49
  5.2 0.6 collective-permute-start.1
  5.9 1.0 collective-permute-start
  6.9 0.7 and_select_fusion
  7.6 3.3 %collective-permute-done.1 = bf16[96,192]{1,0:T(8,128)(2,1)S(1)} collective-permute-done((bf16[96,192]{1,0:T(8,128)(2,1)S(1)}, bf16[96,192]{1,0:T(8,128)(2,1)S(1)}, u32[]{:S(2)}, u32[]{:S(2)}) %collective-permute-start.1) | collective-permute-done | bytes 36896 | tf_op jit(solution)/shard_map/ppermute | solution.py:49
  11.4 0.6 gather_fusion
  12.1 5.9 %collective-permute-start.4 = (bf16[384,192]{0,1:T(8,128)(2,1)S(1)}, bf16[384,192]{0,1:T(8,128)(2,1)S(1)}, u32[]{:S(2)}, u32[]{:S(2)}) collective-permute-start(bf16[384,192]{0,1:T(8,128)(2,1)S(1)} %copy.32), channel_id=1, source_target_pairs={{0,56},{8,0},{16,8},{24,16},{32,24},{40,32},{48,40},{56,48},{1,49}... | collective-permute-start | bytes 442376 | tf_op jit(solution)/shard_map/ppermute | solution.py:63
  18.2 3.8 %collective-permute-done.4 = bf16[384,192]{0,1:T(8,128)(2,1)S(1)} collective-permute-done((bf16[384,192]{0,1:T(8,128)(2,1)S(1)}, bf16[384,192]{0,1:T(8,128)(2,1)S(1)}, u32[]{:S(2)}, u32[]{:S(2)}) %collective-permute-start.4) | collective-permute-done | bytes 147488 | tf_op jit(solution)/shard_map/ppermute | solution.py:63
  22.1 0.7 collective-permute-start.7
  22.8 3.1 %collective-permute-done.3 = bf16[384,192]{0,1:T(8,128)(2,1)S(1)} collective-permute-done((bf16[384,192]{0,1:T(8,128)(2,1)S(1)}, bf16[384,192]{0,1:T(8,128)(2,1)S(1)}, u32[]{:S(2)}, u32[]{:S(2)}) %collective-permute-start.3) | collective-permute-done | bytes 147488 | tf_op jit(solution)/shard_map/ppermute | solution.py:62
  25.9 0.7 collective-permute-start.6
  26.6 1.3 %collective-permute-start.5 = (bf16[384,192]{0,1:T(8,128)(2,1)S(1)}, bf16[384,192]{0,1:T(8,128)(2,1)S(1)}, u32[]{:S(2)}, u32[]{:S(2)}) collective-permute-start(bf16[384,192]{0,1:T(8,128)(2,1)S(1)} %collective-permute-done.3), channel_id=1, source_target_pairs={{1,8},{9,16},{17,24},{25,32},{33,40},{41,48},{49,56},{57,0},{3,10}... | collective-permute-start | bytes 442376 | tf_op jit(solution)/shard_map/ppermute | solution.py:64
  27.9 1.3 %collective-permute-start.8 = (bf16[384,192]{0,1:T(8,128)(2,1)S(1)}, bf16[384,192]{0,1:T(8,128)(2,1)S(1)}, u32[]{:S(2)}, u32[]{:S(2)}) collective-permute-start(bf16[384,192]{0,1:T(8,128)(2,1)S(1)} %collective-permute-done.4), channel_id=1, source_target_pairs={{1,56},{9,0},{17,8},{25,16},{33,24},{41,32},{49,40},{57,48},{3,58}... | collective-permute-start | bytes 442376 | tf_op jit(solution)/shard_map/ppermute | solution.py:70
  29.2 5.0 %collective-permute-done.5 = bf16[384,192]{0,1:T(8,128)(2,1)S(1)} collective-permute-done((bf16[384,192]{0,1:T(8,128)(2,1)S(1)}, bf16[384,192]{0,1:T(8,128)(2,1)S(1)}, u32[]{:S(2)}, u32[]{:S(2)}) %collective-permute-start.5) | collective-permute-done | bytes 147488 | tf_op jit(solution)/shard_map/ppermute | solution.py:64
  34.5 1.0 collective-permute-start.9
  35.7 1.4 %collective-permute-done.9 = bf16[4,384,192]{1,2,0:T(8,128)(2,1)S(1)} collective-permute-done((bf16[4,384,192]{1,2,0:T(8,128)(2,1)S(1)}, bf16[4,384,192]{1,2,0:T(8,128)(2,1)S(1)}, u32[]{:S(2)}, u32[]{:S(2)}) %collective-permute-start.9) | collective-permute-done | bytes 589856 | tf_op jit(solution)/shard_map/ppermute | solution.py:73
  37.8 0.6 gather_fusion.2
  38.5 0.6 gather_fusion.1
  39.1 9.7 %bitcast_convert_fusion = bf16[196,24,192]{0,2,1:T(8,128)(2,1)} fusion(bf16[10,128,192]{1,2,0:T(8,128)(2,1)S(1)} %gather_fusion.1, bf16[10,128,192]{1,2,0:T(8,128)(2,1)S(1)} %gather_fusion.2, bf16[1,1,10,24,128,128]{5,4,3,2,1,0:T(8,128)(2,1)} %param.4), kind=kOutput, calls=%fused_computation.9 | convolution fusion | flops 3828860928 | bytes 10653696 | tf_op jit(solution)/shard_map/tai,tarj->irj/dot_general | solution.py:103
  48.8 3.9 %copy.38 = bf16[196,24,192]{2,1,0:T(8,128)(2,1)S(1)} copy(bf16[196,24,192]{0,2,1:T(8,128)(2,1)} %bitcast_convert_fusion) | data formatting | bytes 3612672 | tf_op jit(solution)/shard_map/convert_element_type | solution.py:103
  52.7 3.2 %gather_fusion.3 = bf16[96,4,24,192]{3,2,1,0:T(8,128)(2,1)} fusion(bf16[49,4,24,192]{3,2,1,0:T(8,128)(2,1)S(1)} %bitcast.81, s32[1024]{0:T(1024)S(1)} %get-tuple-element.9), kind=kCustom, calls=%fused_computation.3 | custom fusion | bytes 7078272 | tf_op jit(solution)/shard_map/jit(_take)/gather | solution.py:109
  55.9 58.3 %all_to_all.18 = bf16[96,1,4,24,192]{4,3,2,1,0:T(8,128)(2,1)S(1)} all-to-all(bf16[96,1,4,24,192]{4,3,2,1,0:T(8,128)(2,1)} %bitcast.82), channel_id=1, replica_groups=mesh['grp'=4,'z'=8,'y'=4,'c'=2] {'grp'}, dimensions={0} | all-to-all | bytes 7077888 | tf_op jit(solution)/shard_map/all_to_all | solution.py:110
  114.3 2.6 %copy.40 = bf16[24,4,4,24,192]{4,3,2,1,0:T(8,128)(2,1)} copy(bf16[24,4,4,24,192]{4,3,2,0,1:T(8,128)(2,1)S(1)} %bitcast.83) | data formatting | bytes 7077888 | tf_op jit(solution)/shard_map/all_to_all | solution.py:110
  (34 shorter events, 2.1 us)
Async XLA Ops:
  0.0 18.1 %copy-start = (s32[48]{0:T(128)S(1)}, s32[48]{0:T(128)}, u32[]{:S(2)}) copy-start(s32[48]{0:T(128)} %param.7) | copy-start | bytes 580
  2.2 5.4 %collective-permute-start.2 = (bf16[96,192]{1,0:T(8,128)(2,1)S(1)}, bf16[96,192]{1,0:T(8,128)(2,1)S(1)}, u32[]{:S(2)}, u32[]{:S(2)}) collective-permute-start(bf16[96,192]{1,0:T(8,128)(2,1)S(1)} %all_gather.3), channel_id=1, source_target_pairs={{0,6},{2,0},{4,2},{6,4},{1,7},{3,1},{5,3},{7,5},{8,14},{10,8},{12,... | collective-permute-start | bytes 110600 | tf_op jit(solution)/shard_map/ppermute | solution.py:49
  5.2 5.6 %collective-permute-start.1 = (bf16[96,192]{1,0:T(8,128)(2,1)S(1)}, bf16[96,192]{1,0:T(8,128)(2,1)S(1)}, u32[]{:S(2)}, u32[]{:S(2)}) collective-permute-start(bf16[96,192]{1,0:T(8,128)(2,1)S(1)} %all_gather.3), channel_id=1, source_target_pairs={{0,4},{2,6},{4,0},{6,2},{1,5},{3,7},{5,1},{7,3},{8,12},{10,14},{12... | collective-permute-start | bytes 110600 | tf_op jit(solution)/shard_map/ppermute | solution.py:49
  5.9 5.5 %collective-permute-start = (bf16[96,192]{1,0:T(8,128)(2,1)S(1)}, bf16[96,192]{1,0:T(8,128)(2,1)S(1)}, u32[]{:S(2)}, u32[]{:S(2)}) collective-permute-start(bf16[96,192]{1,0:T(8,128)(2,1)S(1)} %all_gather.3), channel_id=1, source_target_pairs={{0,2},{2,4},{4,6},{6,0},{1,3},{3,5},{5,7},{7,1},{8,10},{10,12},{12... | collective-permute-start | bytes 110600 | tf_op jit(solution)/shard_map/ppermute | solution.py:49
  12.1 9.9 %collective-permute-start.4 = (bf16[384,192]{0,1:T(8,128)(2,1)S(1)}, bf16[384,192]{0,1:T(8,128)(2,1)S(1)}, u32[]{:S(2)}, u32[]{:S(2)}) collective-permute-start(bf16[384,192]{0,1:T(8,128)(2,1)S(1)} %copy.32), channel_id=1, source_target_pairs={{0,56},{8,0},{16,8},{24,16},{32,24},{40,32},{48,40},{56,48},{1,49}... | collective-permute-start | bytes 442376 | tf_op jit(solution)/shard_map/ppermute | solution.py:63
  18.1 7.8 %collective-permute-start.3 = (bf16[384,192]{0,1:T(8,128)(2,1)S(1)}, bf16[384,192]{0,1:T(8,128)(2,1)S(1)}, u32[]{:S(2)}, u32[]{:S(2)}) collective-permute-start(bf16[384,192]{0,1:T(8,128)(2,1)S(1)} %copy.32), channel_id=1, source_target_pairs={{0,8},{8,16},{16,24},{24,32},{32,40},{40,48},{48,56},{56,0},{1,17}... | collective-permute-start | bytes 442376 | tf_op jit(solution)/shard_map/ppermute | solution.py:62
  22.1 7.1 %collective-permute-start.7 = (bf16[192,192]{0,1:T(8,128)(2,1)S(1)}, bf16[192,192]{0,1:T(8,128)(2,1)S(1)}, u32[]{:S(2)}, u32[]{:S(2)}) collective-permute-start(bf16[192,192]{0,1:T(8,128)(2,1)S(1)} %slice.53), channel_id=1, source_target_pairs={{1,49},{9,57},{17,1},{25,9},{33,17},{41,25},{49,33},{57,41},{3,51}... | collective-permute-start | bytes 221192 | tf_op jit(solution)/shard_map/ppermute | solution.py:68
  25.9 3.3 %collective-permute-start.6 = (bf16[192,192]{0,1:T(8,128)(2,1)S(1)}, bf16[192,192]{0,1:T(8,128)(2,1)S(1)}, u32[]{:S(2)}, u32[]{:S(2)}) collective-permute-start(bf16[192,192]{0,1:T(8,128)(2,1)S(1)} %slice.52), channel_id=1, source_target_pairs={{1,17},{9,25},{17,33},{25,41},{33,49},{41,57},{49,1},{57,9},{3,19}... | collective-permute-start | bytes 221192 | tf_op jit(solution)/shard_map/ppermute | solution.py:67
  26.6 7.7 %collective-permute-start.5 = (bf16[384,192]{0,1:T(8,128)(2,1)S(1)}, bf16[384,192]{0,1:T(8,128)(2,1)S(1)}, u32[]{:S(2)}, u32[]{:S(2)}) collective-permute-start(bf16[384,192]{0,1:T(8,128)(2,1)S(1)} %collective-permute-done.3), channel_id=1, source_target_pairs={{1,8},{9,16},{17,24},{25,32},{33,40},{41,48},{49,56},{57,0},{3,10}... | collective-permute-start | bytes 442376 | tf_op jit(solution)/shard_map/ppermute | solution.py:64
  27.9 6.5 %collective-permute-start.8 = (bf16[384,192]{0,1:T(8,128)(2,1)S(1)}, bf16[384,192]{0,1:T(8,128)(2,1)S(1)}, u32[]{:S(2)}, u32[]{:S(2)}) collective-permute-start(bf16[384,192]{0,1:T(8,128)(2,1)S(1)} %collective-permute-done.4), channel_id=1, source_target_pairs={{1,56},{9,0},{17,8},{25,16},{33,24},{41,32},{49,40},{57,48},{3,58}... | collective-permute-start | bytes 442376 | tf_op jit(solution)/shard_map/ppermute | solution.py:70
  34.5 2.6 %collective-permute-start.9 = (bf16[4,384,192]{1,2,0:T(8,128)(2,1)S(1)}, bf16[4,384,192]{1,2,0:T(8,128)(2,1)S(1)}, u32[]{:S(2)}, u32[]{:S(2)}) collective-permute-start(bf16[4,384,192]{1,2,0:T(8,128)(2,1)S(1)} %pad_maximum_fusion), channel_id=1, source_target_pairs={{0,1},{1,0},{2,3},{3,2},{4,5},{5,4},{6,7},{7,6},{8,9},{9,8},{10,11... | collective-permute-start | bytes 1769480 | tf_op jit(solution)/shard_map/ppermute | solution.py:73

commit v7 on v5

--- a/solution.py
+++ b/solution.py
@@ -73,8 +73,10 @@
 
 
 def gather_coef(coefficients):
-    x = lax.all_gather(coefficients, "c", axis=0, tiled=True)
-    x = direct(x, "y").reshape(-1, NMO)
+    mine = direct(coefficients, "y")
+    theirs = lax.ppermute(mine, "c", [(0, 1), (1, 0)])
+    first = lax.axis_index("c") == 0
+    x = jnp.stack([jnp.where(first, mine, theirs), jnp.where(first, theirs, mine)], axis=1).reshape(-1, NMO)
     if lax.axis_size("z") == 8:
         rows, lo = zring8(x)
     else:

time: 116 us -> 120 us (1.034)
  the two profiles are of different devices: /device:TPU:32 before, /device:TPU:2 now
where the time goes in v7:
time: 120 us; the launch traced here: 119 us
  blocking collectives  58.1 us (48%)
  waiting for transfers between devices  20.4 us (17%)
  starting transfers between devices  14.7 us (12%)
  local copies, waits for them, and re-layouts  13.2 us (11%)
  matrix products  9.67 us (8%)
  other arithmetic  2.37 us (2%)
    all_to_all x1, blocking collectives, body(): return lax.all_to_all(picked[:, None], 'grp', 0, 1, tiled=True)  58.1 us
    dot_general x1, matrix products, body(): jnp.einsum('tai,tarj->irj', la_coef, quarter, preferred_element_type=jnp....  9.67 us
    ppermute x1, waiting for transfers between devices, zring8(): pa = lax.ppermute(f1, zc, [(at(z, 1), at(z + 1, 0)) for z in range(nz)])  7.48 us
    ppermute x1, waiting for transfers between devices, zring8(): lax.ppermute(x, zc, [(at(z, 0), at(z + 1, 0)) for z in range(nz)] + [(at(...  7.04 us
    ppermute x3, starting transfers between devices, direct(): lax.ppermute(x, axis, [(s, (s + o) % n) for s in range(n)])  5.22 us
    ppermute x1, starting transfers between devices, zring8(): lax.ppermute(x, zc, [(at(z, 0), at(z - 1, 0)) for z in range(nz)] + [(at(...  4.04 us
    convert_element_type x1, local copies, waits for them, and re-layouts, body(): jnp.einsum('tai,tarj->irj', la_coef, quarter, preferred_element_type=jnp....  3.87 us
    ppermute x3, waiting for transfers between devices, direct(): lax.ppermute(x, axis, [(s, (s + o) % n) for s in range(n)])  3.52 us
  transfers between devices with their start and end apart: 10, of which 6 were waited for; matrix products, arithmetic and copies ran while one was open for 1% of the time, Pallas kernels for 0%

profile of v7, /device:TPU:2, one launch (start us, length us, event | category | flops | bytes accessed | tf_op | source)
XLA Modules:
  0.0 118.7 jit_solution(11150701830849167004)
XLA Ops:
  0.0 1.6 %collective-permute-start = (bf16[48,192]{1,0:T(8,128)(2,1)}, bf16[48,192]{1,0:T(8,128)(2,1)S(1)}, u32[]{:S(2)}, u32[]{:S(2)}) collective-permute-start(bf16[48,192]{1,0:T(8,128)(2,1)} %param.5), channel_id=1, source_target_pairs={{0,2},{2,4},{4,6},{6,0},{1,3},{3,5},{5,7},{7,1},{8,10},{10,12},{12... | collective-permute-start | bytes 55304 | tf_op jit(solution)/shard_map/ppermute | solution.py:49
  1.6 1.7 %collective-permute-start.2 = (bf16[48,192]{1,0:T(8,128)(2,1)}, bf16[48,192]{1,0:T(8,128)(2,1)S(1)}, u32[]{:S(2)}, u32[]{:S(2)}) collective-permute-start(bf16[48,192]{1,0:T(8,128)(2,1)} %param.5), channel_id=1, source_target_pairs={{0,6},{2,0},{4,2},{6,4},{1,7},{3,1},{5,3},{7,5},{8,14},{10,8},{12,... | collective-permute-start | bytes 55304 | tf_op jit(solution)/shard_map/ppermute | solution.py:49
  3.2 2.0 %collective-permute-start.1 = (bf16[48,192]{1,0:T(8,128)(2,1)}, bf16[48,192]{1,0:T(8,128)(2,1)S(1)}, u32[]{:S(2)}, u32[]{:S(2)}) collective-permute-start(bf16[48,192]{1,0:T(8,128)(2,1)} %param.5), channel_id=1, source_target_pairs={{0,4},{2,6},{4,0},{6,2},{1,5},{3,7},{5,1},{7,3},{8,12},{10,14},{12... | collective-permute-start | bytes 55304 | tf_op jit(solution)/shard_map/ppermute | solution.py:49
  5.6 3.2 %collective-permute-done.1 = bf16[48,192]{1,0:T(8,128)(2,1)S(1)} collective-permute-done((bf16[48,192]{1,0:T(8,128)(2,1)}, bf16[48,192]{1,0:T(8,128)(2,1)S(1)}, u32[]{:S(2)}, u32[]{:S(2)}) %collective-permute-start.1) | collective-permute-done | bytes 18464 | tf_op jit(solution)/shard_map/ppermute | solution.py:49
  8.8 0.8 pad_maximum_fusion.2
  9.5 0.6 gather_fusion
  10.2 0.7 and_select_fusion
  10.9 0.6 collective-permute-done.3
  11.6 2.0 %collective-permute-start.4 = (bf16[384,192]{1,0:T(8,128)(2,1)S(1)}, bf16[384,192]{1,0:T(8,128)(2,1)S(1)}, u32[]{:S(2)}, u32[]{:S(2)}) collective-permute-start(bf16[384,192]{1,0:T(8,128)(2,1)S(1)} %bitcast.85), channel_id=1, source_target_pairs={{0,8},{8,16},{16,24},{24,32},{32,40},{40,48},{48,56},{56,0},{1,17}... | collective-permute-start | bytes 442376 | tf_op jit(solution)/shard_map/ppermute | solution.py:62
  13.8 4.0 %collective-permute-start.5 = (bf16[384,192]{1,0:T(8,128)(2,1)S(1)}, bf16[384,192]{1,0:T(8,128)(2,1)S(1)}, u32[]{:S(2)}, u32[]{:S(2)}) collective-permute-start(bf16[384,192]{1,0:T(8,128)(2,1)S(1)} %bitcast.86), channel_id=1, source_target_pairs={{0,56},{8,0},{16,8},{24,16},{32,24},{40,32},{48,40},{56,48},{1,49}... | collective-permute-start | bytes 442376 | tf_op jit(solution)/shard_map/ppermute | solution.py:63
  17.8 7.0 %collective-permute-done.4 = bf16[384,192]{1,0:T(8,128)(2,1)S(1)} collective-permute-done((bf16[384,192]{1,0:T(8,128)(2,1)S(1)}, bf16[384,192]{1,0:T(8,128)(2,1)S(1)}, u32[]{:S(2)}, u32[]{:S(2)}) %collective-permute-start.4) | collective-permute-done | bytes 147488 | tf_op jit(solution)/shard_map/ppermute | solution.py:62
  24.8 0.7 collective-permute-start.7
  25.5 1.3 %collective-permute-start.6 = (bf16[384,192]{1,0:T(8,128)(2,1)S(1)}, bf16[384,192]{1,0:T(8,128)(2,1)S(1)}, u32[]{:S(2)}, u32[]{:S(2)}) collective-permute-start(bf16[384,192]{1,0:T(8,128)(2,1)S(1)} %collective-permute-done.4), channel_id=1, source_target_pairs={{1,8},{9,16},{17,24},{25,32},{33,40},{41,48},{49,56},{57,0},{3,10}... | collective-permute-start | bytes 442376 | tf_op jit(solution)/shard_map/ppermute | solution.py:64
  26.8 1.3 %collective-permute-start.8 = (bf16[384,192]{1,0:T(8,128)(2,1)S(1)}, bf16[384,192]{1,0:T(8,128)(2,1)S(1)}, u32[]{:S(2)}, u32[]{:S(2)}) collective-permute-start(bf16[384,192]{1,0:T(8,128)(2,1)S(1)} %collective-permute-done.5), channel_id=1, source_target_pairs={{1,56},{9,0},{17,8},{25,16},{33,24},{41,32},{49,40},{57,48},{3,58}... | collective-permute-start | bytes 442376 | tf_op jit(solution)/shard_map/ppermute | solution.py:66
  28.1 7.5 %collective-permute-done.6 = bf16[384,192]{1,0:T(8,128)(2,1)S(1)} collective-permute-done((bf16[384,192]{1,0:T(8,128)(2,1)S(1)}, bf16[384,192]{1,0:T(8,128)(2,1)S(1)}, u32[]{:S(2)}, u32[]{:S(2)}) %collective-permute-start.6) | collective-permute-done | bytes 147488 | tf_op jit(solution)/shard_map/ppermute | solution.py:64
  36.5 1.8 %collective-permute-done.9 = bf16[4,384,192]{1,2,0:T(8,128)(2,1)S(1)} collective-permute-done((bf16[4,384,192]{1,2,0:T(8,128)(2,1)S(1)}, bf16[4,384,192]{1,2,0:T(8,128)(2,1)S(1)}, u32[]{:S(2)}, u32[]{:S(2)}) %collective-permute-start.9) | collective-permute-done | bytes 589856 | tf_op jit(solution)/shard_map/ppermute | solution.py:69
  39.0 0.8 copy.38
  39.9 0.6 gather_fusion.2
  40.5 0.6 gather_fusion.1
  41.2 9.7 %bitcast_convert_fusion = bf16[196,24,192]{0,2,1:T(8,128)(2,1)} fusion(bf16[10,128,192]{1,2,0:T(8,128)(2,1)S(1)} %gather_fusion.1, bf16[10,128,192]{1,2,0:T(8,128)(2,1)S(1)} %gather_fusion.2, bf16[1,1,10,24,128,128]{5,4,3,2,1,0:T(8,128)(2,1)} %param.4), kind=kOutput, calls=%fused_computation.9 | convolution fusion | flops 3828860928 | bytes 10653696 | tf_op jit(solution)/shard_map/tai,tarj->irj/dot_general | solution.py:101
  50.8 3.9 %copy.41 = bf16[196,24,192]{2,1,0:T(8,128)(2,1)S(1)} copy(bf16[196,24,192]{0,2,1:T(8,128)(2,1)} %bitcast_convert_fusion) | data formatting | bytes 3612672 | tf_op jit(solution)/shard_map/convert_element_type | solution.py:101
  54.7 3.2 %gather_fusion.3 = bf16[96,4,24,192]{3,2,1,0:T(8,128)(2,1)} fusion(bf16[49,4,24,192]{3,2,1,0:T(8,128)(2,1)S(1)} %bitcast.81, s32[1024]{0:T(1024)S(1)} %get-tuple-element.11), kind=kCustom, calls=%fused_computation.3 | custom fusion | bytes 7078272 | tf_op jit(solution)/shard_map/jit(_take)/gather | solution.py:107
  58.0 58.1 %all_to_all.18 = bf16[96,1,4,24,192]{4,3,2,1,0:T(8,128)(2,1)S(1)} all-to-all(bf16[96,1,4,24,192]{4,3,2,1,0:T(8,128)(2,1)} %bitcast.82), channel_id=1, replica_groups=mesh['grp'=4,'z'=8,'y'=4,'c'=2] {'grp'}, dimensions={0} | all-to-all | bytes 7077888 | tf_op jit(solution)/shard_map/all_to_all | solution.py:108
  116.0 2.6 %copy.43 = bf16[24,4,4,24,192]{4,3,2,1,0:T(8,128)(2,1)} copy(bf16[24,4,4,24,192]{4,3,2,0,1:T(8,128)(2,1)S(1)} %bitcast.83) | data formatting | bytes 7077888 | tf_op jit(solution)/shard_map/all_to_all | solution.py:108
  (35 shorter events, 2.2 us)
Async XLA Ops:
  0.0 13.6 %copy-start = (s32[48]{0:T(128)S(1)}, s32[48]{0:T(128)}, u32[]{:S(2)}) copy-start(s32[48]{0:T(128)} %param.7) | copy-start | bytes 580
  0.0 5.2 %collective-permute-start = (bf16[48,192]{1,0:T(8,128)(2,1)}, bf16[48,192]{1,0:T(8,128)(2,1)S(1)}, u32[]{:S(2)}, u32[]{:S(2)}) collective-permute-start(bf16[48,192]{1,0:T(8,128)(2,1)} %param.5), channel_id=1, source_target_pairs={{0,2},{2,4},{4,6},{6,0},{1,3},{3,5},{5,7},{7,1},{8,10},{10,12},{12... | collective-permute-start | bytes 55304 | tf_op jit(solution)/shard_map/ppermute | solution.py:49
  1.6 4.0 %collective-permute-start.2 = (bf16[48,192]{1,0:T(8,128)(2,1)}, bf16[48,192]{1,0:T(8,128)(2,1)S(1)}, u32[]{:S(2)}, u32[]{:S(2)}) collective-permute-start(bf16[48,192]{1,0:T(8,128)(2,1)} %param.5), channel_id=1, source_target_pairs={{0,6},{2,0},{4,2},{6,4},{1,7},{3,1},{5,3},{7,5},{8,14},{10,8},{12,... | collective-permute-start | bytes 55304 | tf_op jit(solution)/shard_map/ppermute | solution.py:49
  3.2 5.5 %collective-permute-start.1 = (bf16[48,192]{1,0:T(8,128)(2,1)}, bf16[48,192]{1,0:T(8,128)(2,1)S(1)}, u32[]{:S(2)}, u32[]{:S(2)}) collective-permute-start(bf16[48,192]{1,0:T(8,128)(2,1)} %param.5), channel_id=1, source_target_pairs={{0,4},{2,6},{4,0},{6,2},{1,5},{3,7},{5,1},{7,3},{8,12},{10,14},{12... | collective-permute-start | bytes 55304 | tf_op jit(solution)/shard_map/ppermute | solution.py:49
  10.1 1.4 %collective-permute-start.3 = (bf16[4,48,192]{2,1,0:T(8,128)(2,1)S(1)}, bf16[4,48,192]{2,1,0:T(8,128)(2,1)S(1)}, u32[]{:S(2)}, u32[]{:S(2)}) collective-permute-start(bf16[4,48,192]{2,1,0:T(8,128)(2,1)S(1)} %gather_fusion), channel_id=1, source_target_pairs={{0,1},{1,0},{2,3},{3,2},{4,5},{5,4},{6,7},{7,6},{8,9},{9,8},{10,11... | collective-permute-start | bytes 221192 | tf_op jit(solution)/shard_map/ppermute | solution.py:77
  11.6 13.3 %collective-permute-start.4 = (bf16[384,192]{1,0:T(8,128)(2,1)S(1)}, bf16[384,192]{1,0:T(8,128)(2,1)S(1)}, u32[]{:S(2)}, u32[]{:S(2)}) collective-permute-start(bf16[384,192]{1,0:T(8,128)(2,1)S(1)} %bitcast.85), channel_id=1, source_target_pairs={{0,8},{8,16},{16,24},{24,32},{32,40},{40,48},{48,56},{56,0},{1,17}... | collective-permute-start | bytes 442376 | tf_op jit(solution)/shard_map/ppermute | solution.py:62
  13.8 13.1 %collective-permute-start.5 = (bf16[384,192]{1,0:T(8,128)(2,1)S(1)}, bf16[384,192]{1,0:T(8,128)(2,1)S(1)}, u32[]{:S(2)}, u32[]{:S(2)}) collective-permute-start(bf16[384,192]{1,0:T(8,128)(2,1)S(1)} %bitcast.86), channel_id=1, source_target_pairs={{0,56},{8,0},{16,8},{24,16},{32,24},{40,32},{48,40},{56,48},{1,49}... | collective-permute-start | bytes 442376 | tf_op jit(solution)/shard_map/ppermute | solution.py:63
  24.8 3.3 %collective-permute-start.7 = (bf16[384,192]{1,0:T(8,128)(2,1)S(1)}, bf16[384,192]{1,0:T(8,128)(2,1)S(1)}, u32[]{:S(2)}, u32[]{:S(2)}) collective-permute-start(bf16[384,192]{1,0:T(8,128)(2,1)S(1)} %collective-permute-done.4), channel_id=1, source_target_pairs={{1,17},{9,25},{17,33},{25,41},{33,49},{41,57},{49,1},{57,9},{3,19}... | collective-permute-start | bytes 442376 | tf_op jit(solution)/shard_map/ppermute | solution.py:65
  25.5 10.1 %collective-permute-start.6 = (bf16[384,192]{1,0:T(8,128)(2,1)S(1)}, bf16[384,192]{1,0:T(8,128)(2,1)S(1)}, u32[]{:S(2)}, u32[]{:S(2)}) collective-permute-start(bf16[384,192]{1,0:T(8,128)(2,1)S(1)} %collective-permute-done.4), channel_id=1, source_target_pairs={{1,8},{9,16},{17,24},{25,32},{33,40},{41,48},{49,56},{57,0},{3,10}... | collective-permute-start | bytes 442376 | tf_op jit(solution)/shard_map/ppermute | solution.py:64
  26.8 8.8 %collective-permute-start.8 = (bf16[384,192]{1,0:T(8,128)(2,1)S(1)}, bf16[384,192]{1,0:T(8,128)(2,1)S(1)}, u32[]{:S(2)}, u32[]{:S(2)}) collective-permute-start(bf16[384,192]{1,0:T(8,128)(2,1)S(1)} %collective-permute-done.5), channel_id=1, source_target_pairs={{1,56},{9,0},{17,8},{25,16},{33,24},{41,32},{49,40},{57,48},{3,58}... | collective-permute-start | bytes 442376 | tf_op jit(solution)/shard_map/ppermute | solution.py:66
  36.2 2.1 %collective-permute-start.9 = (bf16[4,384,192]{1,2,0:T(8,128)(2,1)S(1)}, bf16[4,384,192]{1,2,0:T(8,128)(2,1)S(1)}, u32[]{:S(2)}, u32[]{:S(2)}) collective-permute-start(bf16[4,384,192]{1,2,0:T(8,128)(2,1)S(1)} %copy.34), channel_id=1, source_target_pairs={{0,1},{1,0},{2,3},{3,2},{4,5},{5,4},{6,7},{7,6},{8,9},{9,8},{10,11... | collective-permute-start | bytes 1769480 | tf_op jit(solution)/shard_map/ppermute | solution.py:69

commit v8 on v5

--- a/solution.py
+++ b/solution.py
@@ -57,14 +57,14 @@
     zc = ("z", "c")
 
     def at(z, c):
-        return (z % nz) * 2 + c
+        return (z % nz) * 2 + (1 - c)
 
     f1 = lax.ppermute(x, zc, [(at(z, 0), at(z + 1, 0)) for z in range(nz)] + [(at(z, 1), at(z + 2, 1)) for z in range(nz)])
     b1 = lax.ppermute(x, zc, [(at(z, 0), at(z - 1, 0)) for z in range(nz)] + [(at(z, 1), at(z - 2, 1)) for z in range(nz)])
     pa = lax.ppermute(f1, zc, [(at(z, 1), at(z + 1, 0)) for z in range(nz)])
     pb = lax.ppermute(f1, zc, [(at(z, 1), at(z + 2, 1)) for z in range(nz)])
     pc = lax.ppermute(b1, zc, [(at(z, 1), at(z - 1, 0)) for z in range(nz)])
-    first = lax.axis_index("c") == 0
+    first = lax.axis_index("c") == 1
     mine = jnp.stack([f1, b1, jnp.where(first, pa, pb), pc])
     theirs = lax.ppermute(mine, "c", [(0, 1), (1, 0)])
     a = jnp.where(first, mine, theirs)

time: 116 us -> 117 us (level)
  the two profiles are of different devices: /device:TPU:32 before, /device:TPU:2 now
where the time goes in v8:
time: 117 us; the launch traced here: 116 us
  blocking collectives  60.5 us (52%)
  starting transfers between devices  20.3 us (17%)
  local copies, waits for them, and re-layouts  12.3 us (11%)
  waiting for transfers between devices  11.5 us (10%)
  matrix products  9.67 us (8%)
  other arithmetic  1.42 us (1%)
    all_to_all x1, blocking collectives, body(): return lax.all_to_all(picked[:, None], 'grp', 0, 1, tiled=True)  58.3 us
    dot_general x1, matrix products, body(): jnp.einsum('tai,tarj->irj', la_coef, quarter, preferred_element_type=jnp....  9.67 us
    ppermute x3, starting transfers between devices, direct(): lax.ppermute(x, axis, [(s, (s + o) % n) for s in range(n)])  4.67 us
    convert_element_type x1, local copies, waits for them, and re-layouts, body(): jnp.einsum('tai,tarj->irj', la_coef, quarter, preferred_element_type=jnp....  3.87 us
    ppermute x3, waiting for transfers between devices, direct(): lax.ppermute(x, axis, [(s, (s + o) % n) for s in range(n)])  3.8 us
    ppermute x1, starting transfers between devices, zring8(): pb = lax.ppermute(f1, zc, [(at(z, 1), at(z + 2, 1)) for z in range(nz)])  3.57 us
    ppermute x1, starting transfers between devices, zring8(): lax.ppermute(x, zc, [(at(z, 0), at(z + 1, 0)) for z in range(nz)] + [(at(...  3.35 us
    ppermute x1, waiting for transfers between devices, zring8(): lax.ppermute(x, zc, [(at(z, 0), at(z + 1, 0)) for z in range(nz)] + [(at(...  3.24 us
  transfers between devices with their start and end apart: 9, of which 5 were waited for; matrix products, arithmetic and copies ran while one was open for 1% of the time, Pallas kernels for 0%

profile of v8, /device:TPU:2, one launch (start us, length us, event | category | flops | bytes accessed | tf_op | source)
XLA Modules:
  0.0 115.8 jit_solution(3257139591943958124)
XLA Ops:
  0.0 2.2 %all_gather.3 = bf16[96,192]{1,0:T(8,128)(2,1)S(1)} all-gather(bf16[48,192]{1,0:T(8,128)(2,1)} %param.5), channel_id=1, replica_groups=mesh['grp'=4,'z'=8,'y'=4,'c'=2] {'c'}, dimensions={0}, use_global_device_ids=true | all-gather | bytes 55296 | tf_op jit(solution)/shard_map/all_gather | solution.py:76
  2.2 3.1 %collective-permute-start.2 = (bf16[96,192]{1,0:T(8,128)(2,1)S(1)}, bf16[96,192]{1,0:T(8,128)(2,1)S(1)}, u32[]{:S(2)}, u32[]{:S(2)}) collective-permute-start(bf16[96,192]{1,0:T(8,128)(2,1)S(1)} %all_gather.3), channel_id=1, source_target_pairs={{0,6},{2,0},{4,2},{6,4},{1,7},{3,1},{5,3},{7,5},{8,14},{10,8},{12,... | collective-permute-start | bytes 110600 | tf_op jit(solution)/shard_map/ppermute | solution.py:49
  5.2 0.6 collective-permute-start.1
  5.9 1.0 collective-permute-start
  6.9 0.7 and_select_fusion
  7.6 3.3 %collective-permute-done.1 = bf16[96,192]{1,0:T(8,128)(2,1)S(1)} collective-permute-done((bf16[96,192]{1,0:T(8,128)(2,1)S(1)}, bf16[96,192]{1,0:T(8,128)(2,1)S(1)}, u32[]{:S(2)}, u32[]{:S(2)}) %collective-permute-start.1) | collective-permute-done | bytes 36896 | tf_op jit(solution)/shard_map/ppermute | solution.py:49
  10.8 0.5 collective-permute-done
  11.4 0.6 gather_fusion
  12.1 3.3 %collective-permute-start.3 = (bf16[384,192]{0,1:T(8,128)(2,1)S(1)}, bf16[384,192]{0,1:T(8,128)(2,1)S(1)}, u32[]{:S(2)}, u32[]{:S(2)}) collective-permute-start(bf16[384,192]{0,1:T(8,128)(2,1)S(1)} %copy.32), channel_id=1, source_target_pairs={{1,9},{9,17},{17,25},{25,33},{33,41},{41,49},{49,57},{57,1},{0,16}... | collective-permute-start | bytes 442376 | tf_op jit(solution)/shard_map/ppermute | solution.py:62
  15.7 3.1 %collective-permute-start.4 = (bf16[384,192]{0,1:T(8,128)(2,1)S(1)}, bf16[384,192]{0,1:T(8,128)(2,1)S(1)}, u32[]{:S(2)}, u32[]{:S(2)}) collective-permute-start(bf16[384,192]{0,1:T(8,128)(2,1)S(1)} %copy.32), channel_id=1, source_target_pairs={{1,57},{9,1},{17,9},{25,17},{33,25},{41,33},{49,41},{57,49},{0,48}... | collective-permute-start | bytes 442376 | tf_op jit(solution)/shard_map/ppermute | solution.py:63
  18.8 3.2 %collective-permute-done.3 = bf16[384,192]{0,1:T(8,128)(2,1)S(1)} collective-permute-done((bf16[384,192]{0,1:T(8,128)(2,1)S(1)}, bf16[384,192]{0,1:T(8,128)(2,1)S(1)}, u32[]{:S(2)}, u32[]{:S(2)}) %collective-permute-start.3) | collective-permute-done | bytes 147488 | tf_op jit(solution)/shard_map/ppermute | solution.py:62
  22.0 3.6 %collective-permute-start.6 = (bf16[384,192]{0,1:T(8,128)(2,1)S(1)}, bf16[384,192]{0,1:T(8,128)(2,1)S(1)}, u32[]{:S(2)}, u32[]{:S(2)}) collective-permute-start(bf16[384,192]{0,1:T(8,128)(2,1)S(1)} %collective-permute-done.3), channel_id=1, source_target_pairs={{0,16},{8,24},{16,32},{24,40},{32,48},{40,56},{48,0},{56,8},{2,18}... | collective-permute-start | bytes 442376 | tf_op jit(solution)/shard_map/ppermute | solution.py:65
  25.6 1.3 %collective-permute-start.5 = (bf16[384,192]{0,1:T(8,128)(2,1)S(1)}, bf16[384,192]{0,1:T(8,128)(2,1)S(1)}, u32[]{:S(2)}, u32[]{:S(2)}) collective-permute-start(bf16[384,192]{0,1:T(8,128)(2,1)S(1)} %collective-permute-done.3), channel_id=1, source_target_pairs={{0,9},{8,17},{16,25},{24,33},{32,41},{40,49},{48,57},{56,1},{2,11}... | collective-permute-start | bytes 442376 | tf_op jit(solution)/shard_map/ppermute | solution.py:64
  26.9 1.3 %collective-permute-start.7 = (bf16[384,192]{0,1:T(8,128)(2,1)S(1)}, bf16[384,192]{0,1:T(8,128)(2,1)S(1)}, u32[]{:S(2)}, u32[]{:S(2)}) collective-permute-start(bf16[384,192]{0,1:T(8,128)(2,1)S(1)} %collective-permute-done.4), channel_id=1, source_target_pairs={{0,57},{8,1},{16,9},{24,17},{32,25},{40,33},{48,41},{56,49},{2,59}... | collective-permute-start | bytes 442376 | tf_op jit(solution)/shard_map/ppermute | solution.py:66
  28.2 3.0 %collective-permute-done.6 = bf16[384,192]{0,1:T(8,128)(2,1)S(1)} collective-permute-done((bf16[384,192]{0,1:T(8,128)(2,1)S(1)}, bf16[384,192]{0,1:T(8,128)(2,1)S(1)}, u32[]{:S(2)}, u32[]{:S(2)}) %collective-permute-start.6) | collective-permute-done | bytes 147488 | tf_op jit(solution)/shard_map/ppermute | solution.py:65
  31.4 3.0 %collective-permute-start.8 = (bf16[4,384,192]{1,2,0:T(8,128)(2,1)S(1)}, bf16[4,384,192]{1,2,0:T(8,128)(2,1)S(1)}, u32[]{:S(2)}, u32[]{:S(2)}) collective-permute-start(bf16[4,384,192]{1,2,0:T(8,128)(2,1)S(1)} %pad_maximum_fusion), channel_id=1, source_target_pairs={{0,1},{1,0},{2,3},{3,2},{4,5},{5,4},{6,7},{7,6},{8,9},{9,8},{10,11... | collective-permute-start | bytes 1769480 | tf_op jit(solution)/shard_map/ppermute | solution.py:69
  34.6 1.4 %collective-permute-done.8 = bf16[4,384,192]{1,2,0:T(8,128)(2,1)S(1)} collective-permute-done((bf16[4,384,192]{1,2,0:T(8,128)(2,1)S(1)}, bf16[4,384,192]{1,2,0:T(8,128)(2,1)S(1)}, u32[]{:S(2)}, u32[]{:S(2)}) %collective-permute-start.8) | collective-permute-done | bytes 589856 | tf_op jit(solution)/shard_map/ppermute | solution.py:69
  36.8 0.6 gather_fusion.2
  37.4 0.6 gather_fusion.1
  38.1 9.7 %bitcast_convert_fusion = bf16[196,24,192]{0,2,1:T(8,128)(2,1)} fusion(bf16[10,128,192]{1,2,0:T(8,128)(2,1)S(1)} %gather_fusion.1, bf16[10,128,192]{1,2,0:T(8,128)(2,1)S(1)} %gather_fusion.2, bf16[1,1,10,24,128,128]{5,4,3,2,1,0:T(8,128)(2,1)} %param.4), kind=kOutput, calls=%fused_computation.9 | convolution fusion | flops 3828860928 | bytes 10653696 | tf_op jit(solution)/shard_map/tai,tarj->irj/dot_general | solution.py:99
  47.7 3.9 %copy.38 = bf16[196,24,192]{2,1,0:T(8,128)(2,1)S(1)} copy(bf16[196,24,192]{0,2,1:T(8,128)(2,1)} %bitcast_convert_fusion) | data formatting | bytes 3612672 | tf_op jit(solution)/shard_map/convert_element_type | solution.py:99
  51.6 3.2 %gather_fusion.3 = bf16[96,4,24,192]{3,2,1,0:T(8,128)(2,1)} fusion(bf16[49,4,24,192]{3,2,1,0:T(8,128)(2,1)S(1)} %bitcast.81, s32[1024]{0:T(1024)S(1)} %get-tuple-element.9), kind=kCustom, calls=%fused_computation.3 | custom fusion | bytes 7078272 | tf_op jit(solution)/shard_map/jit(_take)/gather | solution.py:105
  54.9 58.3 %all_to_all.18 = bf16[96,1,4,24,192]{4,3,2,1,0:T(8,128)(2,1)S(1)} all-to-all(bf16[96,1,4,24,192]{4,3,2,1,0:T(8,128)(2,1)} %bitcast.82), channel_id=1, replica_groups=mesh['grp'=4,'z'=8,'y'=4,'c'=2] {'grp'}, dimensions={0} | all-to-all | bytes 7077888 | tf_op jit(solution)/shard_map/all_to_all | solution.py:106
  113.2 2.6 %copy.40 = bf16[24,4,4,24,192]{4,3,2,1,0:T(8,128)(2,1)} copy(bf16[24,4,4,24,192]{4,3,2,0,1:T(8,128)(2,1)S(1)} %bitcast.83) | data formatting | bytes 7077888 | tf_op jit(solution)/shard_map/all_to_all | solution.py:106
  (30 shorter events, 1.4 us)
Async XLA Ops:
  0.0 15.5 %copy-start = (s32[48]{0:T(128)S(1)}, s32[48]{0:T(128)}, u32[]{:S(2)}) copy-start(s32[48]{0:T(128)} %param.7) | copy-start | bytes 580
  2.2 5.4 %collective-permute-start.2 = (bf16[96,192]{1,0:T(8,128)(2,1)S(1)}, bf16[96,192]{1,0:T(8,128)(2,1)S(1)}, u32[]{:S(2)}, u32[]{:S(2)}) collective-permute-start(bf16[96,192]{1,0:T(8,128)(2,1)S(1)} %all_gather.3), channel_id=1, source_target_pairs={{0,6},{2,0},{4,2},{6,4},{1,7},{3,1},{5,3},{7,5},{8,14},{10,8},{12,... | collective-permute-start | bytes 110600 | tf_op jit(solution)/shard_map/ppermute | solution.py:49
  5.2 5.6 %collective-permute-start.1 = (bf16[96,192]{1,0:T(8,128)(2,1)S(1)}, bf16[96,192]{1,0:T(8,128)(2,1)S(1)}, u32[]{:S(2)}, u32[]{:S(2)}) collective-permute-start(bf16[96,192]{1,0:T(8,128)(2,1)S(1)} %all_gather.3), channel_id=1, source_target_pairs={{0,4},{2,6},{4,0},{6,2},{1,5},{3,7},{5,1},{7,3},{8,12},{10,14},{12... | collective-permute-start | bytes 110600 | tf_op jit(solution)/shard_map/ppermute | solution.py:49
  5.9 5.5 %collective-permute-start = (bf16[96,192]{1,0:T(8,128)(2,1)S(1)}, bf16[96,192]{1,0:T(8,128)(2,1)S(1)}, u32[]{:S(2)}, u32[]{:S(2)}) collective-permute-start(bf16[96,192]{1,0:T(8,128)(2,1)S(1)} %all_gather.3), channel_id=1, source_target_pairs={{0,2},{2,4},{4,6},{6,0},{1,3},{3,5},{5,7},{7,1},{8,10},{10,12},{12... | collective-permute-start | bytes 110600 | tf_op jit(solution)/shard_map/ppermute | solution.py:49
  12.1 9.9 %collective-permute-start.3 = (bf16[384,192]{0,1:T(8,128)(2,1)S(1)}, bf16[384,192]{0,1:T(8,128)(2,1)S(1)}, u32[]{:S(2)}, u32[]{:S(2)}) collective-permute-start(bf16[384,192]{0,1:T(8,128)(2,1)S(1)} %copy.32), channel_id=1, source_target_pairs={{1,9},{9,17},{17,25},{25,33},{33,41},{41,49},{49,57},{57,1},{0,16}... | collective-permute-start | bytes 442376 | tf_op jit(solution)/shard_map/ppermute | solution.py:62
  15.7 11.3 %collective-permute-start.4 = (bf16[384,192]{0,1:T(8,128)(2,1)S(1)}, bf16[384,192]{0,1:T(8,128)(2,1)S(1)}, u32[]{:S(2)}, u32[]{:S(2)}) collective-permute-start(bf16[384,192]{0,1:T(8,128)(2,1)S(1)} %copy.32), channel_id=1, source_target_pairs={{1,57},{9,1},{17,9},{25,17},{33,25},{41,33},{49,41},{57,49},{0,48}... | collective-permute-start | bytes 442376 | tf_op jit(solution)/shard_map/ppermute | solution.py:63
  22.0 9.2 %collective-permute-start.6 = (bf16[384,192]{0,1:T(8,128)(2,1)S(1)}, bf16[384,192]{0,1:T(8,128)(2,1)S(1)}, u32[]{:S(2)}, u32[]{:S(2)}) collective-permute-start(bf16[384,192]{0,1:T(8,128)(2,1)S(1)} %collective-permute-done.3), channel_id=1, source_target_pairs={{0,16},{8,24},{16,32},{24,40},{32,48},{40,56},{48,0},{56,8},{2,18}... | collective-permute-start | bytes 442376 | tf_op jit(solution)/shard_map/ppermute | solution.py:65
  25.6 5.7 %collective-permute-start.5 = (bf16[384,192]{0,1:T(8,128)(2,1)S(1)}, bf16[384,192]{0,1:T(8,128)(2,1)S(1)}, u32[]{:S(2)}, u32[]{:S(2)}) collective-permute-start(bf16[384,192]{0,1:T(8,128)(2,1)S(1)} %collective-permute-done.3), channel_id=1, source_target_pairs={{0,9},{8,17},{16,25},{24,33},{32,41},{40,49},{48,57},{56,1},{2,11}... | collective-permute-start | bytes 442376 | tf_op jit(solution)/shard_map/ppermute | solution.py:64
  26.9 4.3 %collective-permute-start.7 = (bf16[384,192]{0,1:T(8,128)(2,1)S(1)}, bf16[384,192]{0,1:T(8,128)(2,1)S(1)}, u32[]{:S(2)}, u32[]{:S(2)}) collective-permute-start(bf16[384,192]{0,1:T(8,128)(2,1)S(1)} %collective-permute-done.4), channel_id=1, source_target_pairs={{0,57},{8,1},{16,9},{24,17},{32,25},{40,33},{48,41},{56,49},{2,59}... | collective-permute-start | bytes 442376 | tf_op jit(solution)/shard_map/ppermute | solution.py:66
  31.4 4.6 %collective-permute-start.8 = (bf16[4,384,192]{1,2,0:T(8,128)(2,1)S(1)}, bf16[4,384,192]{1,2,0:T(8,128)(2,1)S(1)}, u32[]{:S(2)}, u32[]{:S(2)}) collective-permute-start(bf16[4,384,192]{1,2,0:T(8,128)(2,1)S(1)} %pad_maximum_fusion), channel_id=1, source_target_pairs={{0,1},{1,0},{2,3},{3,2},{4,5},{5,4},{6,7},{7,6},{8,9},{9,8},{10,11... | collective-permute-start | bytes 1769480 | tf_op jit(solution)/shard_map/ppermute | solution.py:69
